TPU v7x, 32 devices: a whole 2x2x4 slice. The times are simulated.
32 devices in a mesh: pipe: 2 (over x), ctx: 8 (over z, y), tp: 2 (over core).
Axes of the slice: x: 2, y: 2, z: 4, core: 2. Of those that a mesh axis runs over, the one named last changes fastest.
Arguments:
- fwd_in: bfloat16 [2, 1024, 3, 8192], P('pipe', 'ctx', None, 'tp'), may hold values from -60 to 60
- bwd_in: bfloat16 [2, 1024, 3, 8192], P('pipe', 'ctx', None, 'tp'), may hold values from -60 to 60
- bwd_cot: bfloat16 [2, 1024, 8192], P('pipe', 'ctx', 'tp'), may hold values from -16 to 16
- filter_taps: float32 [2, 2, 4096, 1024], P('pipe', 'tp', 'ctx'), may hold values from -8 to 8
- norm_gain: float32 [2, 8192], P('pipe', 'tp'), may hold values from 0.5 to 2
Outputs:
- next_rows: bfloat16 [2, 1024, 8192], P('pipe', 'ctx', 'tp')
- prev_grads: bfloat16 [2, 1024, 3, 8192], P('pipe', 'ctx', None, 'tp')
- taps_grad: float32 [2, 2, 4096, 1024], P('pipe', 'tp', 'ctx')
All inputs are finite; a program needn't handle non-finite values.
Results may differ from a plain program's by a relative error of at most 0.0058.
Values may be sent and summed in bfloat16 or wider, within the bound.
No kernel may reach another device: no remote copies, remote signals or barrier semaphores. Data moves between devices by JAX's collectives and lax.ppermute only.
A program may use at most 128 MiB of HBM per device.

v0:
```python
import math

import jax
import jax.numpy as jnp
from jax import lax
from jax.sharding import PartitionSpec as P

epsilon = 1e-06
highest = lax.Precision.HIGHEST


def from_partner(block, axis, bit):
    count = lax.axis_size(axis)
    route = []
    for low in range(count):
        high = low | 1 << bit
        if high != low and high < count:
            route += [(low, high), (high, low)]
    return lax.ppermute(block, axis, route)


def unit_table(count_out, count_in, period):
    product = lax.broadcasted_iota(jnp.int32, (count_out, count_in), 0) * lax.broadcasted_iota(
        jnp.int32, (count_out, count_in), 1
    )
    phase_angle = (product % period).astype(jnp.float32) * (-2.0 * math.pi / period)
    return (jnp.cos(phase_angle), jnp.sin(phase_angle))


def dft_tables(padded):
    blocks = padded // 128
    cos_high, sin_high = unit_table(blocks, blocks, blocks)
    cos_low, sin_low = unit_table(128, 128, 128)
    cos_twist, sin_twist = unit_table(blocks, 128, padded)
    return (cos_high, sin_high, cos_low, sin_low, cos_twist, sin_twist)


def spectrum(signal, tables):
    cos_high, sin_high, cos_low, sin_low, cos_twist, sin_twist = tables
    channels = signal.shape[0]
    half_blocks = signal.shape[1] // 128
    folded = signal.reshape(channels, half_blocks, 128)
    first_re = jnp.einsum("can,ak->ckn", folded, cos_high[:half_blocks], precision=highest)
    first_im = jnp.einsum("can,ak->ckn", folded, sin_high[:half_blocks], precision=highest)
    turned_re = first_re * cos_twist - first_im * sin_twist
    turned_im = first_re * sin_twist + first_im * cos_twist
    spec_re = jnp.einsum("ckn,nj->ckj", turned_re, cos_low, precision=highest) - jnp.einsum(
        "ckn,nj->ckj", turned_im, sin_low, precision=highest
    )
    spec_im = jnp.einsum("ckn,nj->ckj", turned_re, sin_low, precision=highest) + jnp.einsum(
        "ckn,nj->ckj", turned_im, cos_low, precision=highest
    )
    return (spec_re, spec_im)


def signal_of(spec_re, spec_im, tables):
    cos_high, sin_high, cos_low, sin_low, cos_twist, sin_twist = tables
    channels = spec_re.shape[0]
    blocks = spec_re.shape[1]
    half_blocks = blocks // 2
    mid_re = jnp.einsum("ckj,jn->ckn", spec_re, cos_low, precision=highest) + jnp.einsum(
        "ckj,jn->ckn", spec_im, sin_low, precision=highest
    )
    mid_im = jnp.einsum("ckj,jn->ckn", spec_im, cos_low, precision=highest) - jnp.einsum(
        "ckj,jn->ckn", spec_re, sin_low, precision=highest
    )
    back_re = mid_re * cos_twist + mid_im * sin_twist
    back_im = mid_im * cos_twist - mid_re * sin_twist
    values = jnp.einsum(
        "ak,ckn->can", cos_high[:half_blocks], back_re, precision=highest
    ) + jnp.einsum("ak,ckn->can", sin_high[:half_blocks], back_im, precision=highest)
    return values.reshape(channels, half_blocks * 128) / (blocks * 128)


def spec_product(a_re, a_im, b_re, b_im):
    return (a_re * b_re - a_im * b_im, a_re * b_im + a_im * b_re)


def spec_against(a_re, a_im, b_re, b_im):
    return (a_re * b_re + a_im * b_im, a_im * b_re - a_re * b_im)


def split_bf16(values):
    high = lax.reduce_precision(values, exponent_bits=8, mantissa_bits=7)
    return (high.astype(jnp.bfloat16), (values - high).astype(jnp.bfloat16))


def unit_angles(count_rows, count_cols, stride, padded):
    rows = lax.broadcasted_iota(jnp.int32, (count_rows, count_cols), 0) * stride
    cols = lax.broadcasted_iota(jnp.int32, (count_rows, count_cols), 1)
    angle = ((rows * cols) % padded).astype(jnp.float32) * (2.0 * math.pi / padded)
    return (jnp.cos(angle), jnp.sin(angle))


def real_dft_table(length):
    padded = 2 * length
    inner = 1 << (length.bit_length() // 2)
    if length % inner:
        inner = 1
    outer = length // inner
    cos_outer, sin_outer = unit_angles(outer, length, inner, padded)
    cos_inner, sin_inner = unit_angles(inner, length, 1, padded)
    cos_full = (cos_outer[:, None] * cos_inner[None] - sin_outer[:, None] * sin_inner[None]).reshape(
        length, length
    )
    sin_full = (sin_outer[:, None] * cos_inner[None] + cos_outer[:, None] * sin_inner[None]).reshape(
        length, length
    )
    rows = lax.broadcasted_iota(jnp.int32, (length, length), 0)
    cols = lax.broadcasted_iota(jnp.int32, (length, length), 1)
    alternating = jnp.where(rows % 2 == 0, 1.0, -1.0).astype(jnp.float32)
    sin_part = jnp.where(cols == 0, alternating, -sin_full)
    table = jnp.concatenate([cos_full, sin_part], axis=1)
    return split_bf16(table)


def dot_tf(table, signal):
    return lax.dot_general(
        table, signal, (((0,), (0,)), ((), ())), preferred_element_type=jnp.float32
    )


def dot_tt(table, spec):
    return lax.dot_general(
        table, spec, (((1,), (0,)), ((), ())), preferred_element_type=jnp.float32
    )


def dense_spectrum_exact(rows_bf16, table):
    table_hi, table_lo = table
    return dot_tf(table_hi, rows_bf16) + dot_tf(table_lo, rows_bf16)


def dense_signal(spec, table):
    table_hi, table_lo = table
    spec_hi, spec_lo = split_bf16(spec)
    return dot_tt(table_hi, spec_hi) + (dot_tt(table_lo, spec_hi) + dot_tt(table_hi, spec_lo))


def dense_taps_spectrum(taps, table):
    table_hi, table_lo = table
    taps_hi, taps_lo = split_bf16(taps)
    dims = (((0,), (1,)), ((), ()))
    part = lambda a, b: lax.dot_general(a, b, dims, preferred_element_type=jnp.float32)
    return part(table_hi, taps_hi) + (part(table_lo, taps_hi) + part(table_hi, taps_lo))


def spectral_weights(length):
    index = lax.broadcasted_iota(jnp.int32, (2 * length, 1), 0)
    edge = (index == 0) | (index == length)
    return jnp.where(edge, 1.0, 2.0).astype(jnp.float32) / (2 * length)


def dense_multiply(a, b, conjugate):
    length = a.shape[0] // 2
    a_re, a_im = a[:length], a[length:]
    b_re, b_im = b[:length], b[length:]
    first = lax.broadcasted_iota(jnp.int32, (length, 1), 0) == 0
    if conjugate:
        re = a_re * b_re + a_im * b_im
        im = a_im * b_re - a_re * b_im
    else:
        re = a_re * b_re - a_im * b_im
        im = a_re * b_im + a_im * b_re
    re = jnp.where(first, a_re * b_re, re)
    im = jnp.where(first, a_im * b_im, im)
    return jnp.concatenate([re, im], axis=0)


def dense_fits(length):
    return 4 * length * length * 2 <= 16 * 1024 * 1024


def on_device_factored(fwd_in, bwd_in, bwd_cot, filter_taps, norm_gain):
    model_width = norm_gain.shape[1] * lax.axis_size("tp")
    local_taps = filter_taps[0, 0]
    tables = dft_tables(2 * local_taps.shape[1])
    tap_re, tap_im = spectrum(local_taps, tables)
    gain_row = norm_gain[0]
    forward_rows = fwd_in[0]
    backward_rows = bwd_in[0]

    def featurize(proj_rows):
        return (proj_rows[:, 1].astype(jnp.float32) * proj_rows[:, 2].astype(jnp.float32)).astype(
            jnp.bfloat16
        )

    def convolve(columns):
        sig_re, sig_im = spectrum(columns.astype(jnp.float32), tables)
        prod_re, prod_im = spec_product(sig_re, sig_im, tap_re, tap_im)
        return (signal_of(prod_re, prod_im, tables).astype(jnp.bfloat16), (sig_re, sig_im))

    def relayout(mixed_rows):
        columns = lax.all_to_all(
            jnp.transpose(mixed_rows), "ctx", split_axis=0, concat_axis=1, tiled=True
        )
        result, kept_spec = convolve(columns)
        return (
            jnp.transpose(lax.all_to_all(result, "ctx", split_axis=1, concat_axis=0, tiled=True)),
            kept_spec,
        )

    def row_total(values):
        return lax.psum(jnp.sum(values, axis=1), "tp")

    forward_mix = featurize(forward_rows)
    backward_mix = featurize(backward_rows)
    forward_z = relayout(forward_mix)[0]
    backward_z, backward_spec = relayout(backward_mix)
    forward_y = forward_rows[:, 0].astype(jnp.float32) * forward_z.astype(jnp.float32)
    backward_q = backward_rows[:, 0].astype(jnp.float32)
    conv_value = backward_z.astype(jnp.float32)
    backward_y = backward_q * conv_value
    weighted = bwd_cot[0].astype(jnp.float32) * gain_row
    forward_scale = lax.rsqrt(row_total(forward_y * forward_y) / model_width + epsilon)[:, None]
    backward_scale = lax.rsqrt(row_total(backward_y * backward_y) / model_width + epsilon)[:, None]
    normed = backward_y * backward_scale
    average = (row_total(weighted * normed) / model_width)[:, None]
    forward_out = (forward_y * forward_scale * gain_row).astype(jnp.bfloat16)
    grad_y = backward_scale * (weighted - normed * average)
    grad_z = (grad_y * backward_q).astype(jnp.bfloat16)
    grad_cols = lax.all_to_all(
        jnp.transpose(grad_z), "ctx", split_axis=0, concat_axis=1, tiled=True
    )
    grad_re, grad_im = spectrum(grad_cols.astype(jnp.float32), tables)
    input_re, input_im = spec_against(grad_re, grad_im, tap_re, tap_im)
    grad_mix_cols = signal_of(input_re, input_im, tables).astype(jnp.bfloat16)
    taps_re, taps_im = spec_against(grad_re, grad_im, backward_spec[0], backward_spec[1])
    filt_step = signal_of(taps_re, taps_im, tables)
    grad_mix = jnp.transpose(
        lax.all_to_all(grad_mix_cols, "ctx", split_axis=1, concat_axis=0, tiled=True)
    ).astype(jnp.float32)
    section_grads = jnp.stack(
        [
            grad_y * conv_value,
            grad_mix * backward_rows[:, 2].astype(jnp.float32),
            grad_mix * backward_rows[:, 1].astype(jnp.float32),
        ],
        axis=1,
    ).astype(jnp.bfloat16)
    section_grads, filt_step = (section_grads, filt_step)
    sent_rows, sent_grads = from_partner((forward_out, section_grads), "pipe", 0)
    return (sent_rows[None], sent_grads[None], filt_step[None, None])


def on_device(fwd_in, bwd_in, bwd_cot, filter_taps, norm_gain):
    length = filter_taps.shape[3]
    if not dense_fits(length):
        return on_device_factored(fwd_in, bwd_in, bwd_cot, filter_taps, norm_gain)
    model_width = norm_gain.shape[1] * lax.axis_size("tp")
    table = real_dft_table(length)
    weights = spectral_weights(length)
    tap_spec = dense_taps_spectrum(filter_taps[0, 0], table)
    tap_scaled = tap_spec * weights
    gain_row = norm_gain[0]
    forward_rows = fwd_in[0]
    backward_rows = bwd_in[0]

    def featurize(proj_rows):
        return (proj_rows[:, 1].astype(jnp.float32) * proj_rows[:, 2].astype(jnp.float32)).astype(
            jnp.bfloat16
        )

    def to_columns(rows):
        return lax.all_to_all(rows, "ctx", split_axis=1, concat_axis=0, tiled=True)

    def to_rows(columns):
        return lax.all_to_all(columns, "ctx", split_axis=0, concat_axis=1, tiled=True)

    def row_total(values):
        return lax.psum(jnp.sum(values, axis=1), "tp")

    partner_kv = from_partner(backward_rows[:, 1:3], "pipe", 0)
    forward_cols = to_columns(featurize(forward_rows))
    backward_cols = to_columns(featurize(backward_rows))
    forward_spec = dense_spectrum_exact(forward_cols, table)
    forward_z = to_rows(
        dense_signal(dense_multiply(forward_spec, tap_scaled, False), table).astype(jnp.bfloat16)
    )
    partner_kv, backward_cols = lax.optimization_barrier((partner_kv, backward_cols))
    backward_spec = dense_spectrum_exact(backward_cols, table)
    backward_z = to_rows(
        dense_signal(dense_multiply(backward_spec, tap_scaled, False), table).astype(jnp.bfloat16)
    )
    forward_y = forward_rows[:, 0].astype(jnp.float32) * forward_z.astype(jnp.float32)
    forward_scale = lax.rsqrt(row_total(forward_y * forward_y) / model_width + epsilon)[:, None]
    forward_out = (forward_y * forward_scale * gain_row).astype(jnp.bfloat16)
    sent_rows = from_partner(forward_out, "pipe", 0)
    backward_q = backward_rows[:, 0].astype(jnp.float32)
    conv_value = backward_z.astype(jnp.float32)
    backward_y = backward_q * conv_value
    weighted = bwd_cot[0].astype(jnp.float32) * gain_row
    backward_scale = lax.rsqrt(row_total(backward_y * backward_y) / model_width + epsilon)[:, None]
    normed = backward_y * backward_scale
    average = (row_total(weighted * normed) / model_width)[:, None]
    grad_y = backward_scale * (weighted - normed * average)
    grad_z = (grad_y * backward_q).astype(jnp.bfloat16)
    sent_first = from_partner((grad_y * conv_value).astype(jnp.bfloat16), "pipe", 0)
    grad_cols = to_columns(grad_z)
    sent_rows, sent_first, grad_cols = lax.optimization_barrier((sent_rows, sent_first, grad_cols))
    grad_spec = dense_spectrum_exact(grad_cols, table) * weights
    grad_mix_cols = dense_signal(dense_multiply(grad_spec, tap_spec, True), table).astype(
        jnp.bfloat16
    )
    taps_prod = dense_multiply(grad_spec, backward_spec, True)
    taps_hi, taps_lo = split_bf16(taps_prod)
    table_hi, table_lo = table
    dims = (((0,), (1,)), ((), ()))
    part = lambda a, b: lax.dot_general(a, b, dims, preferred_element_type=jnp.float32)
    filt_step = part(taps_hi, table_hi) + (part(taps_hi, table_lo) + part(taps_lo, table_hi))
    sent_mix = from_partner(to_rows(grad_mix_cols), "pipe", 0).astype(jnp.float32)
    rest = jnp.stack(
        [
            sent_mix * partner_kv[:, 1].astype(jnp.float32),
            sent_mix * partner_kv[:, 0].astype(jnp.float32),
        ],
        axis=1,
    ).astype(jnp.bfloat16)
    sent_grads = jnp.concatenate([sent_first[:, None], rest], axis=1)
    return (sent_rows[None], sent_grads[None], filt_step[None, None])


def solution(mesh):
    return jax.shard_map(
        on_device,
        mesh=mesh,
        in_specs=(
            P("pipe", "ctx", None, "tp"),
            P("pipe", "ctx", None, "tp"),
            P("pipe", "ctx", "tp"),
            P("pipe", "tp", "ctx", None),
            P("pipe", "tp"),
        ),
        out_specs=(
            P("pipe", "ctx", "tp"),
            P("pipe", "ctx", None, "tp"),
            P("pipe", "tp", "ctx", None),
        ),
        check_vma=False,
    )
```

profile of v0, /device:TPU:0, one launch (start us, length us, event | category | flops | bytes accessed | tf_op | source)
XLA Modules:
  0.0 310.0 jit_solution(16255534303952740677)
XLA Ops:
  0.6 3.5 %copy.23 = bf16[1,128,3,4096]{1,3,2,0:T(8,128)(2,1)S(1)} copy(bf16[1,128,3,4096]{3,1,2,0:T(8,128)(2,1)} %param.6) | data formatting | bytes 6291456 | tf_op args[1]
  4.1 1.5 slice.90
  5.6 2.9 collective-permute-start.1
  9.8 5.8 %all-to-all-start.2 = ((bf16[128,8,512]{0,2,1:T(8,128)(2,1)}), bf16[128,8,512]{0,2,1:T(8,128)(2,1)}, u32[]{:S(2)}, u32[]{:S(2)}) async-start(bf16[128,8,512]{0,2,1:T(8,128)(2,1)} %bitcast.130), calls=%async_computation.2 | async-start | bytes 2097152 | tf_op jit(solution)/shard_map/all_to_all | solution.py:265
  16.7 4.5 %multiply_subtract_fusion = (f32[32,32,1024]{2,1,0:T(8,128)}, f32[32,32,1024]{2,1,0:T(8,128)}) fusion(f32[32,1024]{1,0:T(8,128)S(1)} %get-tuple-element.42, f32[32,1024]{1,0:T(8,128)S(1)} %get-tuple-element.39, f32[32,1024]{1,0:T(8,128)S(1)} %get-tuple-element.43, f32[32,1024]{1,0:T(8,128)S(1)} %get-tuple-element.38), kind=kLoop, calls=%fused_computation.25 | loop fusion | flops 7340032 | bytes 8912896 | tf_op jit(solution)/shard_map/sub | solution.py:103
  21.2 4.6 %copy.20 = bf16[1,128,3,4096]{1,3,2,0:T(8,128)(2,1)} copy(bf16[1,128,3,4096]{3,1,2,0:T(8,128)(2,1)} %param.5) | data formatting | bytes 6291456 | tf_op args[0]
  25.9 2.8 bitcast_select_fusion
  29.3 4.2 %fusion = (bf16[1024,2048]{1,0:T(8,128)(2,1)}, bf16[1024,2048]{1,0:T(8,128)(2,1)}) fusion(f32[1024,1024]{1,0:T(8,128)S(1)} %bitcast_select_fusion, f32[1024,1024]{1,0:T(8,128)S(1)} %bitcast.128), kind=kLoop, calls=%fused_computation.2 | loop fusion | flops 10485760 | bytes 16777216 | tf_op jit(solution)/shard_map/convert_element_type | solution.py:85
  34.7 6.6 %all-to-all-done.2 = bf16[128,8,512]{0,2,1:T(8,128)(2,1)} async-done(((bf16[128,8,512]{0,2,1:T(8,128)(2,1)}), bf16[128,8,512]{0,2,1:T(8,128)(2,1)}, u32[]{:S(2)}, u32[]{:S(2)}) %all-to-all-start.2) | async-done | bytes 1048608 | tf_op jit(solution)/shard_map/all_to_all | solution.py:265
  41.3 4.6 %all-to-all-start = ((bf16[128,8,512]{0,2,1:T(8,128)(2,1)}), bf16[128,8,512]{0,2,1:T(8,128)(2,1)}, u32[]{:S(2)}, u32[]{:S(2)}) async-start(bf16[128,8,512]{0,2,1:T(8,128)(2,1)} %bitcast.131), calls=%async_computation | async-start | bytes 2097152 | tf_op jit(solution)/shard_map/all_to_all | solution.py:265
  45.9 5.5 %fusion.29 = f32[2048,512]{1,0:T(8,128)S(1)} fusion(bf16[1024,2048]{1,0:T(8,128)(2,1)} %get-tuple-element.27, f32[1,1,512,1024]{3,2,1,0:T(8,128)} %param.8), kind=kOutput, calls=%fused_computation.76 | convolution fusion | flops 2148532224 | bytes 10485760 | tf_op jit(solution)/shard_map/dot_general | solution.py:144
  51.4 2.4 fusion.28
  53.9 6.6 %broadcast_multiply_fusion = (f32[2048,512]{1,0:T(8,128)}, f32[2048,512]{1,0:T(8,128)}) fusion(f32[2048]{0:T(1024)S(1)} %select_multiply_fusion, f32[2048,512]{1,0:T(8,128)S(1)} %fusion.29, f32[2048,512]{1,0:T(8,128)S(1)} %fusion.28, bf16[1024,2048]{1,0:T(8,128)(2,1)S(1)} %copy-done, f32[1,1,512,1024]{3,2,1,0:T(8,128)S(1)} %copy-done.17), kind=kOutput, calls=%fused_computation.65 | convolution fusion | flops 2152202240 | bytes 23076864 | tf_op jit(solution)/shard_map/dot_general | solution.py:144
  60.5 2.3 copy.24
  62.7 8.6 %all-to-all-done = bf16[128,8,512]{0,2,1:T(8,128)(2,1)} async-done(((bf16[128,8,512]{0,2,1:T(8,128)(2,1)}), bf16[128,8,512]{0,2,1:T(8,128)(2,1)}, u32[]{:S(2)}, u32[]{:S(2)}) %all-to-all-start) | async-done | bytes 1048608 | tf_op jit(solution)/shard_map/all_to_all | solution.py:265
  71.3 2.8 copy.21
  74.1 5.1 %fusion.71 = f32[2048,512]{1,0:T(8,128)S(1)} fusion(bf16[1024,2048]{1,0:T(8,128)(2,1)} %get-tuple-element.27, bf16[1024,512]{1,0:T(8,128)(2,1)} %bitcast.140), kind=kOutput, calls=%fused_computation.133 | convolution fusion | flops 2147483648 | bytes 9437184 | tf_op jit(solution)/shard_map/dot_general | solution.py:118
  79.2 2.4 convolution_add_fusion.1
  81.7 2.4 fusion.72
  84.1 2.5 convolution_add_fusion
  86.7 3.4 %subtract_select_fusion = (f32[1024,512]{1,0:T(8,128)S(1)}, f32[1024,512]{1,0:T(8,128)S(1)}, f32[1024,512]{1,0:T(8,128)}, f32[1024,512]{1,0:T(8,128)}) fusion(f32[2048,512]{1,0:T(8,128)S(1)} %convolution_add_fusion, f32[2048,512]{1,0:T(8,128)S(1)} %copy-done.5, pred[1024]{0:T(1024)(128)(4,1)S(1)} %get-tuple-element.46, f32[2048,512]{1,0:T(8,128)S(1)} %convolution_add_fusion.1), kind=kLoop, calls=%fused_computation.29 | loop fusion | flops 8388608 | bytes 20972544 | tf_op jit(solution)/shard_map/jit(_where)/select_n | solution.py:165
  90.1 2.3 fusion.48
  92.5 2.3 fusion.49
  94.8 3.3 %add_convert_fusion.1 = bf16[1024,512]{1,0:T(8,128)(2,1)} fusion(f32[1024,512]{1,0:T(8,128)S(1)} %fusion.49, f32[1024,512]{1,0:T(8,128)S(1)} %fusion.48, bf16[1024,2048]{1,0:T(8,128)(2,1)S(1)} %copy-done.1, f32[1024,512]{1,0:T(8,128)S(1)} %get-tuple-element.23, f32[1024,512]{1,0:T(8,128)S(1)} %get-tuple-element.22), kind=kOutput, calls=%fused_computation.58 | convolution fusion | flops 2153250816 | bytes 13631488 | tf_op jit(solution)/shard_map/dot_general | solution.py:124
  98.1 4.3 %all-to-all-start.3 = ((bf16[8,128,512]{2,1,0:T(8,128)(2,1)}), bf16[8,128,512]{2,1,0:T(8,128)(2,1)}, u32[]{:S(2)}, u32[]{:S(2)}) async-start(bf16[8,128,512]{2,1,0:T(8,128)(2,1)} %bitcast.137), calls=%async_computation.3 | async-start | bytes 2097152 | tf_op jit(solution)/shard_map/all_to_all | solution.py:268
  102.4 5.9 %fusion.46 = f32[1024,512]{1,0:T(8,128)S(1)} fusion(bf16[1024,2048]{1,0:T(8,128)(2,1)} %get-tuple-element.26, f32[1024,512]{1,0:T(8,128)} %get-tuple-element.30, f32[1024,512]{1,0:T(8,128)} %get-tuple-element.31), kind=kOutput, calls=%fused_computation.99 | convolution fusion | flops 2150629376 | bytes 10485760 | tf_op jit(solution)/shard_map/dot_general | solution.py:124
  108.4 2.3 fusion.47
  110.7 3.4 %add_convert_fusion.2 = bf16[1024,512]{1,0:T(8,128)(2,1)} fusion(f32[1024,512]{1,0:T(8,128)S(1)} %fusion.47, f32[1024,512]{1,0:T(8,128)S(1)} %fusion.46, bf16[1024,2048]{1,0:T(8,128)(2,1)S(1)} %copy-done.2, f32[1024,512]{1,0:T(8,128)S(1)} %copy-done.15, f32[1024,512]{1,0:T(8,128)S(1)} %copy-done.16), kind=kOutput, calls=%fused_computation.63 | convolution fusion | flops 2153250816 | bytes 13631488 | tf_op jit(solution)/shard_map/dot_general | solution.py:124
  114.0 13.7 %all-to-all-done.3 = bf16[8,128,512]{2,1,0:T(8,128)(2,1)} async-done(((bf16[8,128,512]{2,1,0:T(8,128)(2,1)}), bf16[8,128,512]{2,1,0:T(8,128)(2,1)}, u32[]{:S(2)}, u32[]{:S(2)}) %all-to-all-start.3) | async-done | bytes 1048608 | tf_op jit(solution)/shard_map/all_to_all | solution.py:268
  127.8 4.2 %all-to-all-start.1 = ((bf16[8,128,512]{2,1,0:T(8,128)(2,1)}), bf16[8,128,512]{2,1,0:T(8,128)(2,1)}, u32[]{:S(2)}, u32[]{:S(2)}) async-start(bf16[8,128,512]{2,1,0:T(8,128)(2,1)} %bitcast.134), calls=%async_computation.1 | async-start | bytes 2097152 | tf_op jit(solution)/shard_map/all_to_all | solution.py:268
  132.0 2.3 copy.26
  134.3 1.5 slice_convert_fusion
  135.7 2.9 copy.28
  138.6 2.7 copy.27
  142.5 2.8 convert_bitcast_fusion
  145.3 2.9 copy.25
  148.2 2.1 multiply_reduce_fusion.1
  150.4 2.5 psum.22
  152.8 4.6 %all-to-all-done.1 = bf16[8,128,512]{2,1,0:T(8,128)(2,1)} async-done(((bf16[8,128,512]{2,1,0:T(8,128)(2,1)}), bf16[8,128,512]{2,1,0:T(8,128)(2,1)}, u32[]{:S(2)}, u32[]{:S(2)}) %all-to-all-start.1) | async-done | bytes 1048608 | tf_op jit(solution)/shard_map/all_to_all | solution.py:268
  157.4 2.8 convert_bitcast_fusion.1
  160.2 2.9 copy.22
  163.2 2.6 multiply_reduce_fusion.2
  166.9 2.5 all-reduce
  169.3 4.3 %multiply_convert_fusion = bf16[128,8,512]{2,0,1:T(8,128)(2,1)} fusion(f32[128,8,512]{2,0,1:T(8,128)} %copy.28, f32[128,8,512]{2,0,1:T(8,128)} %copy.27, f32[128]{0:T(128)S(1)} %broadcast_multiply_fusion.1, f32[8,512]{1,0:T(8,128)S(1)} %mul.340, f32[128]{0:T(128)S(1)} %add_rsqrt_fusion, bf16[8,128,512]{2,1,0:T(8,128)(2,1)} %all-to-all-done.3), kind=kLoop, calls=%fused_computation.55 | loop fusion | flops 4718592 | bytes 6308864 | tf_op jit(solution)/shard_map/convert_element_type | solution.py:297
  173.6 4.7 %all-to-all-start.4 = ((bf16[128,8,512]{2,0,1:T(8,128)(2,1)}), bf16[128,8,512]{2,0,1:T(8,128)(2,1)}, u32[]{:S(2)}, u32[]{:S(2)}) async-start(bf16[128,8,512]{2,0,1:T(8,128)(2,1)} %multiply_convert_fusion), calls=%async_computation.4 | async-start | bytes 2097152 | tf_op jit(solution)/shard_map/all_to_all | solution.py:265
  178.3 3.3 %fusion.16 = (bf16[128,4096]{0,1:T(8,128)(2,1)S(1)}, bf16[128,4096]{0,1:T(8,128)(2,1)S(1)}) fusion(f32[128,8,512]{0,2,1:T(8,128)} %copy.25, bf16[1,128,4096]{1,2,0:T(8,128)(2,1)} %copy.26, f32[128]{0:T(128)S(1)} %broadcast_multiply_fusion.1, f32[128]{0:T(128)S(1)} %add_rsqrt_fusion, f32[4096]{0:T(1024)S(1)} %bitcast.144, ...), kind=kLoop, calls=%fused_computation.48 | loop fusion | flops 7864320 | bytes 9455104 | tf_op jit(solution)/shard_map/convert_element_type | solution.py:298
  182.3 1.5 collective-permute-start.2
  183.8 24.0 %collective-permute-done = bf16[128,4096]{0,1:T(8,128)(2,1)S(1)} collective-permute-done((bf16[128,4096]{0,1:T(8,128)(2,1)S(1)}, bf16[128,4096]{0,1:T(8,128)(2,1)S(1)}, u32[]{:S(2)}, u32[]{:S(2)}) %collective-permute-start) | collective-permute-done | bytes 1048608 | tf_op jit(solution)/shard_map/ppermute | solution.py:19
  207.7 21.7 %collective-permute-done.2 = bf16[128,4096]{0,1:T(8,128)(2,1)S(1)} collective-permute-done((bf16[128,4096]{0,1:T(8,128)(2,1)S(1)}, bf16[128,4096]{0,1:T(8,128)(2,1)S(1)}, u32[]{:S(2)}, u32[]{:S(2)}) %collective-permute-start.2) | collective-permute-done | bytes 1048608 | tf_op jit(solution)/shard_map/ppermute | solution.py:19
  229.4 5.4 %fusion.73 = f32[2048,512]{1,0:T(8,128)S(1)} fusion(bf16[1024,2048]{1,0:T(8,128)(2,1)} %get-tuple-element.26, bf16[1024,512]{1,0:T(8,128)(2,1)} %bitcast.24), kind=kOutput, calls=%fused_computation.135 | convolution fusion | flops 2147483648 | bytes 9437184 | tf_op jit(solution)/shard_map/dot_general | solution.py:118
  234.9 3.8 %add_multiply_fusion = f32[2048,512]{1,0:T(8,128)S(1)} fusion(f32[2048,512]{1,0:T(8,128)S(1)} %fusion.73, bf16[1024,2048]{1,0:T(8,128)(2,1)S(1)} %copy-done.3, bf16[1024,512]{1,0:T(8,128)(2,1)} %bitcast.24, f32[2048]{0:T(1024)S(1)} %select_multiply_fusion), kind=kOutput, calls=%fused_computation.21 | convolution fusion | flops 2149580800 | bytes 13639680 | tf_op jit(solution)/shard_map/dot_general | solution.py:118
  238.7 2.6 add_select_fusion
  241.3 2.3 fusion.50
  243.6 2.3 fusion.51
  246.0 3.3 %add_convert_fusion = bf16[1024,512]{1,0:T(8,128)(2,1)} fusion(f32[1024,512]{1,0:T(8,128)S(1)} %fusion.51, f32[1024,512]{1,0:T(8,128)S(1)} %fusion.50, bf16[1024,2048]{1,0:T(8,128)(2,1)S(1)} %copy-done.3, f32[1024,512]{1,0:T(8,128)S(1)} %get-tuple-element.28, f32[1024,512]{1,0:T(8,128)S(1)} %get-tuple-element.29), kind=kOutput, calls=%fused_computation.53 | convolution fusion | flops 2153250816 | bytes 13631488 | tf_op jit(solution)/shard_map/dot_general | solution.py:124
  249.3 5.9 %all-to-all-start.5 = ((bf16[8,128,512]{2,1,0:T(8,128)(2,1)}), bf16[8,128,512]{2,1,0:T(8,128)(2,1)S(1)}, u32[]{:S(2)}, u32[]{:S(2)}) async-start(bf16[8,128,512]{2,1,0:T(8,128)(2,1)} %bitcast.139), calls=%async_computation.5 | async-start | bytes 2097152 | tf_op jit(solution)/shard_map/all_to_all | solution.py:268
  255.2 6.6 %fusion.52 = f32[512,1024]{1,0:T(8,128)} fusion(bf16[1024,2048]{1,0:T(8,128)(2,1)} %get-tuple-element.26, f32[1024,512]{1,0:T(8,128)} %get-tuple-element.19, f32[1024,512]{1,0:T(8,128)S(1)} %get-tuple-element.18), kind=kOutput, calls=%fused_computation.105 | convolution fusion | flops 2150629376 | bytes 10485760 | tf_op jit(solution)/shard_map/dot_general | solution.py:309
  261.8 18.5 %all-to-all-done.5 = bf16[8,128,512]{2,1,0:T(8,128)(2,1)S(1)} async-done(((bf16[8,128,512]{2,1,0:T(8,128)(2,1)}), bf16[8,128,512]{2,1,0:T(8,128)(2,1)S(1)}, u32[]{:S(2)}, u32[]{:S(2)}) %all-to-all-start.5) | async-done | bytes 1048608 | tf_op jit(solution)/shard_map/all_to_all | solution.py:268
  282.1 6.5 %fusion.53 = f32[512,1024]{1,0:T(8,128)} fusion(bf16[1024,2048]{1,0:T(8,128)(2,1)} %get-tuple-element.27, f32[1024,512]{1,0:T(8,128)} %get-tuple-element.19, f32[1024,512]{1,0:T(8,128)S(1)} %get-tuple-element.18), kind=kOutput, calls=%fused_computation.106 | convolution fusion | flops 2150629376 | bytes 10485760 | tf_op jit(solution)/shard_map/dot_general | solution.py:309
  288.6 2.3 copy.31
  290.9 7.8 %add_bitcast_fusion = f32[1,1,512,1024]{3,2,1,0:T(8,128)} fusion(f32[512,1024]{1,0:T(8,128)} %fusion.53, f32[512,1024]{1,0:T(8,128)} %fusion.52, bf16[1024,2048]{1,0:T(8,128)(2,1)} %get-tuple-element.27, f32[1024,512]{1,0:T(8,128)} %get-tuple-element.19, f32[1024,512]{1,0:T(8,128)S(1)} %get-tuple-element.18), kind=kOutput, calls=%fused_computation.51 | convolution fusion | flops 2152726528 | bytes 14680064 | tf_op jit(solution)/shard_map/dot_general | solution.py:309
  298.7 5.9 %collective-permute-done.3 = bf16[128,4096]{0,1:T(8,128)(2,1)S(1)} collective-permute-done((bf16[128,4096]{0,1:T(8,128)(2,1)}, bf16[128,4096]{0,1:T(8,128)(2,1)S(1)}, u32[]{:S(2)}, u32[]{:S(2)}) %collective-permute-start.3) | collective-permute-done | bytes 1048608 | tf_op jit(solution)/shard_map/ppermute | solution.py:19
  304.6 2.0 fusion.27
  307.0 2.8 copy.32
  (69 shorter events, 9.4 us)
Async XLA Ops:
  5.6 76.1 %collective-permute-start.1 = (bf16[128,2,4096]{0,2,1:T(8,128)(2,1)}, bf16[128,2,4096]{0,2,1:T(8,128)(2,1)}, u32[]{:S(2)}, u32[]{:S(2)}) collective-permute-start(bf16[128,2,4096]{0,2,1:T(8,128)(2,1)} %slice.90), channel_id=1, source_target_pairs={{0,16},{16,0},{1,17},{17,1},{2,18},{18,2},{3,19},{19,3},{4,20},{20... | collective-permute-start | bytes 6291464 | tf_op jit(solution)/shard_map/ppermute | solution.py:19
  9.8 31.6 %all-to-all-start.2 = ((bf16[128,8,512]{0,2,1:T(8,128)(2,1)}), bf16[128,8,512]{0,2,1:T(8,128)(2,1)}, u32[]{:S(2)}, u32[]{:S(2)}) async-start(bf16[128,8,512]{0,2,1:T(8,128)(2,1)} %bitcast.130), calls=%async_computation.2 | async-start | bytes 2097152 | tf_op jit(solution)/shard_map/all_to_all | solution.py:265
  25.9 3.4 %copy-start.9 = (f32[32,32,1024]{2,1,0:T(8,128)S(1)}, f32[32,32,1024]{2,1,0:T(8,128)}, u32[]{:S(2)}) copy-start(f32[32,32,1024]{2,1,0:T(8,128)} %get-tuple-element.34) | copy-start | bytes 12582916
  29.3 4.2 %copy-start.7 = (bf16[1,128,3,4096]{1,3,2,0:T(8,128)(2,1)S(1)}, bf16[1,128,3,4096]{1,3,2,0:T(8,128)(2,1)}, u32[]{:S(2)}) copy-start(bf16[1,128,3,4096]{1,3,2,0:T(8,128)(2,1)} %copy.20) | copy-start | bytes 9437188
  41.3 30.0 %all-to-all-start = ((bf16[128,8,512]{0,2,1:T(8,128)(2,1)}), bf16[128,8,512]{0,2,1:T(8,128)(2,1)}, u32[]{:S(2)}, u32[]{:S(2)}) async-start(bf16[128,8,512]{0,2,1:T(8,128)(2,1)} %bitcast.131), calls=%async_computation | async-start | bytes 2097152 | tf_op jit(solution)/shard_map/all_to_all | solution.py:265
  45.9 5.5 %copy-start.12 = (bf16[1024,2048]{1,0:T(8,128)(2,1)S(1)}, bf16[1024,2048]{1,0:T(8,128)(2,1)}, u32[]{:S(2)}) copy-start(bf16[1024,2048]{1,0:T(8,128)(2,1)} %get-tuple-element.26) | copy-start | bytes 12582916
  45.9 5.5 %copy-start.17 = (f32[1,1,512,1024]{3,2,1,0:T(8,128)S(1)}, f32[1,1,512,1024]{3,2,1,0:T(8,128)}, u32[]{:S(2)}) copy-start(f32[1,1,512,1024]{3,2,1,0:T(8,128)} %param.8) | copy-start | bytes 6291460
  51.4 2.4 copy-start
  74.1 5.1 %copy-start.13 = (bf16[1024,2048]{1,0:T(8,128)(2,1)S(1)}, bf16[1024,2048]{1,0:T(8,128)(2,1)}, u32[]{:S(2)}) copy-start(bf16[1024,2048]{1,0:T(8,128)(2,1)} %get-tuple-element.26) | copy-start | bytes 12582916
  74.1 5.1 %copy-start.20 = (bf16[8,128,512]{2,1,0:T(8,128)(2,1)S(1)}, bf16[8,128,512]{2,1,0:T(8,128)(2,1)}, u32[]{:S(2)}) copy-start(bf16[8,128,512]{2,1,0:T(8,128)(2,1)} %copy.21) | copy-start | bytes 3145732
  79.2 2.4 copy-start.19
  81.6 2.5 copy-start.1
  84.1 2.6 copy-start.5
  86.7 3.5 %copy-start.10 = (f32[2048,512]{1,0:T(8,128)}, f32[2048,512]{1,0:T(8,128)S(1)}, u32[]{:S(2)}) copy-start(f32[2048,512]{1,0:T(8,128)S(1)} %convolution_add_fusion) | copy-start | bytes 12582916
  98.1 29.7 %all-to-all-start.3 = ((bf16[8,128,512]{2,1,0:T(8,128)(2,1)}), bf16[8,128,512]{2,1,0:T(8,128)(2,1)}, u32[]{:S(2)}, u32[]{:S(2)}) async-start(bf16[8,128,512]{2,1,0:T(8,128)(2,1)} %bitcast.137), calls=%async_computation.3 | async-start | bytes 2097152 | tf_op jit(solution)/shard_map/all_to_all | solution.py:268
  102.4 6.0 %copy-start.2 = (bf16[1024,2048]{1,0:T(8,128)(2,1)S(1)}, bf16[1024,2048]{1,0:T(8,128)(2,1)}, u32[]{:S(2)}) copy-start(bf16[1024,2048]{1,0:T(8,128)(2,1)} %get-tuple-element.27) | copy-start | bytes 12582916
  102.4 6.0 %copy-start.15 = (f32[1024,512]{1,0:T(8,128)S(1)}, f32[1024,512]{1,0:T(8,128)}, u32[]{:S(2)}) copy-start(f32[1024,512]{1,0:T(8,128)} %get-tuple-element.30) | copy-start | bytes 6291460
  102.4 6.0 %copy-start.16 = (f32[1024,512]{1,0:T(8,128)S(1)}, f32[1024,512]{1,0:T(8,128)}, u32[]{:S(2)}) copy-start(f32[1024,512]{1,0:T(8,128)} %get-tuple-element.31) | copy-start | bytes 6291460
  127.8 29.6 %all-to-all-start.1 = ((bf16[8,128,512]{2,1,0:T(8,128)(2,1)}), bf16[8,128,512]{2,1,0:T(8,128)(2,1)}, u32[]{:S(2)}, u32[]{:S(2)}) async-start(bf16[8,128,512]{2,1,0:T(8,128)(2,1)} %bitcast.134), calls=%async_computation.1 | async-start | bytes 2097152 | tf_op jit(solution)/shard_map/all_to_all | solution.py:268
  138.6 3.2 %copy-start.23 = (f32[1,4096]{1,0:T(1,128)S(1)}, f32[1,4096]{1,0:T(1,128)}, u32[]{:S(2)}) copy-start(f32[1,4096]{1,0:T(1,128)} %param.9) | copy-start | bytes 49156
  163.2 2.6 copy-start.6
  163.2 2.8 copy-start.8
  173.6 55.8 %all-to-all-start.4 = ((bf16[128,8,512]{2,0,1:T(8,128)(2,1)}), bf16[128,8,512]{2,0,1:T(8,128)(2,1)}, u32[]{:S(2)}, u32[]{:S(2)}) async-start(bf16[128,8,512]{2,0,1:T(8,128)(2,1)} %multiply_convert_fusion), calls=%async_computation.4 | async-start | bytes 2097152 | tf_op jit(solution)/shard_map/all_to_all | solution.py:265
  181.7 26.1 %collective-permute-start = (bf16[128,4096]{0,1:T(8,128)(2,1)S(1)}, bf16[128,4096]{0,1:T(8,128)(2,1)S(1)}, u32[]{:S(2)}, u32[]{:S(2)}) collective-permute-start(bf16[128,4096]{0,1:T(8,128)(2,1)S(1)} %get-tuple-element.37), channel_id=1, source_target_pairs={{0,16},{16,0},{1,17},{17,1},{2,18},{18,2},{3,19},{19,3},{4,20},{20... | collective-permute-start | bytes 3145736 | tf_op jit(solution)/shard_map/ppermute | solution.py:19
  182.3 47.2 %collective-permute-start.2 = (bf16[128,4096]{0,1:T(8,128)(2,1)S(1)}, bf16[128,4096]{0,1:T(8,128)(2,1)S(1)}, u32[]{:S(2)}, u32[]{:S(2)}) collective-permute-start(bf16[128,4096]{0,1:T(8,128)(2,1)S(1)} %get-tuple-element.36), channel_id=1, source_target_pairs={{0,16},{16,0},{1,17},{17,1},{2,18},{18,2},{3,19},{19,3},{4,20},{20... | collective-permute-start | bytes 3145736 | tf_op jit(solution)/shard_map/ppermute | solution.py:19
  207.7 27.1 %copy-start.18 = (bf16[128,4096]{0,1:T(8,128)(2,1)}, bf16[128,4096]{0,1:T(8,128)(2,1)S(1)}, u32[]{:S(2)}) copy-start(bf16[128,4096]{0,1:T(8,128)(2,1)S(1)} %collective-permute-done) | copy-start | bytes 3145732
  229.4 5.4 %copy-start.21 = (bf16[128,4096]{0,1:T(8,128)(2,1)}, bf16[128,4096]{0,1:T(8,128)(2,1)S(1)}, u32[]{:S(2)}) copy-start(bf16[128,4096]{0,1:T(8,128)(2,1)S(1)} %collective-permute-done.2) | copy-start | bytes 3145732
  229.4 5.4 %copy-start.3 = (bf16[1024,2048]{1,0:T(8,128)(2,1)S(1)}, bf16[1024,2048]{1,0:T(8,128)(2,1)}, u32[]{:S(2)}) copy-start(bf16[1024,2048]{1,0:T(8,128)(2,1)} %get-tuple-element.27) | copy-start | bytes 12582916
  234.8 3.8 %copy-start.4 = (f32[2048,512]{1,0:T(8,128)S(1)}, f32[2048,512]{1,0:T(8,128)}, u32[]{:S(2)}) copy-start(f32[2048,512]{1,0:T(8,128)} %get-tuple-element.41) | copy-start | bytes 12582916
  234.9 3.8 %copy-start.11 = (f32[2048,512]{1,0:T(8,128)S(1)}, f32[2048,512]{1,0:T(8,128)}, u32[]{:S(2)}) copy-start(f32[2048,512]{1,0:T(8,128)} %copy-done.10) | copy-start | bytes 12582916
  238.7 2.6 copy-start.14
  249.3 31.0 %all-to-all-start.5 = ((bf16[8,128,512]{2,1,0:T(8,128)(2,1)}), bf16[8,128,512]{2,1,0:T(8,128)(2,1)S(1)}, u32[]{:S(2)}, u32[]{:S(2)}) async-start(bf16[8,128,512]{2,1,0:T(8,128)(2,1)} %bitcast.139), calls=%async_computation.5 | async-start | bytes 2097152 | tf_op jit(solution)/shard_map/all_to_all | solution.py:268
  281.6 23.0 %collective-permute-start.3 = (bf16[128,4096]{0,1:T(8,128)(2,1)}, bf16[128,4096]{0,1:T(8,128)(2,1)S(1)}, u32[]{:S(2)}, u32[]{:S(2)}) collective-permute-start(bf16[128,4096]{0,1:T(8,128)(2,1)} %bitcast.138), channel_id=1, source_target_pairs={{0,16},{16,0},{1,17},{17,1},{2,18},{18,2},{3,19},{19,3},{4,20},{20... | collective-permute-start | bytes 3145736 | tf_op jit(solution)/shard_map/ppermute | solution.py:19
  298.7 8.0 %copy-start.22 = (bf16[128,4096]{0,1:T(8,128)(2,1)S(1)}, bf16[128,4096]{0,1:T(8,128)(2,1)}, u32[]{:S(2)}) copy-start(bf16[128,4096]{0,1:T(8,128)(2,1)} %copy-done.21) | copy-start | bytes 3145732
where the time goes:
time: 315 us; the launch traced here: 310 us
  waiting for transfers between devices  104 us (33%)
  matrix products  84.5 us (27%)
  other arithmetic  44.6 us (14%)
  local copies, waits for them, and re-layouts  36 us (11%)
  starting transfers between devices  35 us (11%)
  blocking collectives  4.93 us (2%)
    ppermute x4, waiting for transfers between devices, from_partner(): return lax.ppermute(block, axis, route)  51.6 us
    all_to_all x3, waiting for transfers between devices, to_rows(): lax.all_to_all(columns, 'ctx', split_axis=0, concat_axis=1, tiled=True)  36.8 us
    dot_general x9, matrix products, dot_tt(): lax.dot_general(table, spec, (((1,), (0,)), ((), ())), preferred_element_...  27.5 us
    dot_general x6, matrix products, dot_tf(): lax.dot_general(table, signal, (((0,), (0,)), ((), ())), preferred_elemen...  21.6 us
    dot_general x3, matrix products, on_device(): lax.dot_general(a, b, dims, preferred_element_type=jnp.float32)  20.9 us
    unnamed x54, local copies, waits for them, and re-layouts  16.8 us
    all_to_all x3, waiting for transfers between devices, to_columns(): return lax.all_to_all(rows, 'ctx', split_axis=1, concat_axis=0, tiled=True)  15.2 us
    all_to_all x3, starting transfers between devices, to_columns(): return lax.all_to_all(rows, 'ctx', split_axis=1, concat_axis=0, tiled=True)  15 us
  transfers between devices with their start and end apart: 10, of which 8 were waited for; matrix products, arithmetic and copies ran while one was open for 33% of the time, Pallas kernels for 0%

commit v1 on v0

--- a/solution.py
+++ b/solution.py
@@ -297,11 +297,11 @@
     grad_z = (grad_y * backward_q).astype(jnp.bfloat16)
     sent_first = from_partner((grad_y * conv_value).astype(jnp.bfloat16), "pipe", 0)
     grad_cols = to_columns(grad_z)
-    sent_rows, sent_first, grad_cols = lax.optimization_barrier((sent_rows, sent_first, grad_cols))
     grad_spec = dense_spectrum_exact(grad_cols, table) * weights
     grad_mix_cols = dense_signal(dense_multiply(grad_spec, tap_spec, True), table).astype(
         jnp.bfloat16
     )
+    sent_rows, sent_first, grad_mix_cols = lax.optimization_barrier((sent_rows, sent_first, grad_mix_cols))
     taps_prod = dense_multiply(grad_spec, backward_spec, True)
     taps_hi, taps_lo = split_bf16(taps_prod)
     table_hi, table_lo = table

time: 315 us -> 302 us (0.959)
  waiting for transfers between devices: 104 us -> 88.9 us
    ppermute x4, waiting for transfers between devices: 51.6 us -> 12.3 us  [from_partner(): return lax.ppermute(block, axis, route)]
    all_to_all x3, waiting for transfers between devices: 15.2 us -> 35.2 us  [to_columns(): return lax.all_to_all(rows, 'ctx', split_axis=1, concat_axis=0, tiled=True)]
    all_to_all x3, waiting for transfers between devices: 36.8 us -> 41.4 us  [to_rows(): lax.all_to_all(columns, 'ctx', split_axis=0, concat_axis=1, tiled=True)]
    unnamed x54 -> x50, local copies, waits for them, and re-layouts: 16.8 us -> 16.6 us
  transfers between devices with their start and end apart: 10 -> 10, of which waited for: 8 -> 8; matrix products, arithmetic and copies ran while one was open for 33% -> 41% of each run, Pallas kernels for 0% -> 0%
where the time goes in v1:
time: 302 us; the launch traced here: 297 us
  waiting for transfers between devices  88.9 us (29%)
  matrix products  84.3 us (28%)
  other arithmetic  46.5 us (15%)
  local copies, waits for them, and re-layouts  35.8 us (12%)
  starting transfers between devices  34.9 us (12%)
  blocking collectives  4.93 us (2%)
    all_to_all x3, waiting for transfers between devices, to_rows(): lax.all_to_all(columns, 'ctx', split_axis=0, concat_axis=1, tiled=True)  41.4 us
    all_to_all x3, waiting for transfers between devices, to_columns(): return lax.all_to_all(rows, 'ctx', split_axis=1, concat_axis=0, tiled=True)  35.2 us
    dot_general x9, matrix products, dot_tt(): lax.dot_general(table, spec, (((1,), (0,)), ((), ())), preferred_element_...  27.6 us
    dot_general x6, matrix products, dot_tf(): lax.dot_general(table, signal, (((0,), (0,)), ((), ())), preferred_elemen...  21.4 us
    dot_general x3, matrix products, on_device(): lax.dot_general(a, b, dims, preferred_element_type=jnp.float32)  20.9 us
    unnamed x50, local copies, waits for them, and re-layouts  16.6 us
    all_to_all x3, starting transfers between devices, to_columns(): return lax.all_to_all(rows, 'ctx', split_axis=1, concat_axis=0, tiled=True)  15 us
    dot_general x3, matrix products, dense_taps_spectrum(): lax.dot_general(a, b, dims, preferred_element_type=jnp.float32)  14.5 us
  transfers between devices with their start and end apart: 10, of which 8 were waited for; matrix products, arithmetic and copies ran while one was open for 41% of the time, Pallas kernels for 0%

profile of v1, /device:TPU:0, one launch (start us, length us, event | category | flops | bytes accessed | tf_op | source)
XLA Modules:
  0.0 296.7 jit_solution(9972062549327762780)
XLA Ops:
  0.6 3.5 %copy.23 = bf16[1,128,3,4096]{1,3,2,0:T(8,128)(2,1)S(1)} copy(bf16[1,128,3,4096]{3,1,2,0:T(8,128)(2,1)} %param.6) | data formatting | bytes 6291456 | tf_op args[1]
  4.1 1.5 slice.90
  5.6 2.9 collective-permute-start.1
  9.8 5.8 %all-to-all-start.2 = ((bf16[128,8,512]{0,2,1:T(8,128)(2,1)}), bf16[128,8,512]{0,2,1:T(8,128)(2,1)}, u32[]{:S(2)}, u32[]{:S(2)}) async-start(bf16[128,8,512]{0,2,1:T(8,128)(2,1)} %bitcast.130), calls=%async_computation.2 | async-start | bytes 2097152 | tf_op jit(solution)/shard_map/all_to_all | solution.py:265
  16.7 4.5 %multiply_subtract_fusion = (f32[32,32,1024]{2,1,0:T(8,128)}, f32[32,32,1024]{2,1,0:T(8,128)}) fusion(f32[32,1024]{1,0:T(8,128)S(1)} %get-tuple-element.42, f32[32,1024]{1,0:T(8,128)S(1)} %get-tuple-element.39, f32[32,1024]{1,0:T(8,128)S(1)} %get-tuple-element.43, f32[32,1024]{1,0:T(8,128)S(1)} %get-tuple-element.38), kind=kLoop, calls=%fused_computation.25 | loop fusion | flops 7340032 | bytes 8912896 | tf_op jit(solution)/shard_map/sub | solution.py:103
  21.2 4.6 %copy.20 = bf16[1,128,3,4096]{1,3,2,0:T(8,128)(2,1)} copy(bf16[1,128,3,4096]{3,1,2,0:T(8,128)(2,1)} %param.5) | data formatting | bytes 6291456 | tf_op args[0]
  25.8 2.8 bitcast_select_fusion
  29.3 4.1 %fusion = (bf16[1024,2048]{1,0:T(8,128)(2,1)}, bf16[1024,2048]{1,0:T(8,128)(2,1)}) fusion(f32[1024,1024]{1,0:T(8,128)S(1)} %bitcast_select_fusion, f32[1024,1024]{1,0:T(8,128)S(1)} %bitcast.128), kind=kLoop, calls=%fused_computation.2 | loop fusion | flops 10485760 | bytes 16777216 | tf_op jit(solution)/shard_map/convert_element_type | solution.py:85
  34.7 6.6 %all-to-all-done.2 = bf16[128,8,512]{0,2,1:T(8,128)(2,1)} async-done(((bf16[128,8,512]{0,2,1:T(8,128)(2,1)}), bf16[128,8,512]{0,2,1:T(8,128)(2,1)}, u32[]{:S(2)}, u32[]{:S(2)}) %all-to-all-start.2) | async-done | bytes 1048608 | tf_op jit(solution)/shard_map/all_to_all | solution.py:265
  41.3 4.5 %all-to-all-start = ((bf16[128,8,512]{0,2,1:T(8,128)(2,1)}), bf16[128,8,512]{0,2,1:T(8,128)(2,1)}, u32[]{:S(2)}, u32[]{:S(2)}) async-start(bf16[128,8,512]{0,2,1:T(8,128)(2,1)} %bitcast.131), calls=%async_computation | async-start | bytes 2097152 | tf_op jit(solution)/shard_map/all_to_all | solution.py:265
  45.9 5.5 %fusion.29 = f32[2048,512]{1,0:T(8,128)S(1)} fusion(bf16[1024,2048]{1,0:T(8,128)(2,1)} %get-tuple-element.27, f32[1,1,512,1024]{3,2,1,0:T(8,128)} %param.8), kind=kOutput, calls=%fused_computation.76 | convolution fusion | flops 2148532224 | bytes 10485760 | tf_op jit(solution)/shard_map/dot_general | solution.py:144
  51.4 2.4 fusion.28
  53.8 6.6 %broadcast_multiply_fusion = (f32[2048,512]{1,0:T(8,128)}, f32[2048,512]{1,0:T(8,128)}) fusion(f32[2048]{0:T(1024)S(1)} %select_multiply_fusion, f32[2048,512]{1,0:T(8,128)S(1)} %fusion.29, f32[2048,512]{1,0:T(8,128)S(1)} %fusion.28, bf16[1024,2048]{1,0:T(8,128)(2,1)S(1)} %copy-done, f32[1,1,512,1024]{3,2,1,0:T(8,128)S(1)} %copy-done.17), kind=kOutput, calls=%fused_computation.65 | convolution fusion | flops 2152202240 | bytes 23076864 | tf_op jit(solution)/shard_map/dot_general | solution.py:144
  60.5 2.3 copy.24
  62.7 8.6 %all-to-all-done = bf16[128,8,512]{0,2,1:T(8,128)(2,1)} async-done(((bf16[128,8,512]{0,2,1:T(8,128)(2,1)}), bf16[128,8,512]{0,2,1:T(8,128)(2,1)}, u32[]{:S(2)}, u32[]{:S(2)}) %all-to-all-start) | async-done | bytes 1048608 | tf_op jit(solution)/shard_map/all_to_all | solution.py:265
  71.3 2.8 copy.21
  74.1 5.1 %fusion.71 = f32[2048,512]{1,0:T(8,128)S(1)} fusion(bf16[1024,2048]{1,0:T(8,128)(2,1)} %get-tuple-element.27, bf16[1024,512]{1,0:T(8,128)(2,1)} %bitcast.140), kind=kOutput, calls=%fused_computation.133 | convolution fusion | flops 2147483648 | bytes 9437184 | tf_op jit(solution)/shard_map/dot_general | solution.py:118
  79.2 2.4 convolution_add_fusion.1
  81.7 2.4 fusion.72
  84.1 2.5 convolution_add_fusion
  86.7 3.4 %subtract_select_fusion = (f32[1024,512]{1,0:T(8,128)S(1)}, f32[1024,512]{1,0:T(8,128)S(1)}, f32[1024,512]{1,0:T(8,128)}, f32[1024,512]{1,0:T(8,128)}) fusion(f32[2048,512]{1,0:T(8,128)S(1)} %convolution_add_fusion, f32[2048,512]{1,0:T(8,128)S(1)} %copy-done.5, pred[1024]{0:T(1024)(128)(4,1)S(1)} %get-tuple-element.46, f32[2048,512]{1,0:T(8,128)S(1)} %convolution_add_fusion.1), kind=kLoop, calls=%fused_computation.29 | loop fusion | flops 8388608 | bytes 20972544 | tf_op jit(solution)/shard_map/jit(_where)/select_n | solution.py:165
  90.1 2.3 fusion.49
  92.5 2.3 fusion.48
  94.8 3.3 %add_convert_fusion.1 = bf16[1024,512]{1,0:T(8,128)(2,1)} fusion(f32[1024,512]{1,0:T(8,128)S(1)} %fusion.49, f32[1024,512]{1,0:T(8,128)S(1)} %fusion.48, bf16[1024,2048]{1,0:T(8,128)(2,1)S(1)} %copy-done.1, f32[1024,512]{1,0:T(8,128)S(1)} %get-tuple-element.23, f32[1024,512]{1,0:T(8,128)S(1)} %get-tuple-element.22), kind=kOutput, calls=%fused_computation.58 | convolution fusion | flops 2153250816 | bytes 13631488 | tf_op jit(solution)/shard_map/dot_general | solution.py:124
  98.1 4.3 %all-to-all-start.3 = ((bf16[8,128,512]{2,1,0:T(8,128)(2,1)}), bf16[8,128,512]{2,1,0:T(8,128)(2,1)}, u32[]{:S(2)}, u32[]{:S(2)}) async-start(bf16[8,128,512]{2,1,0:T(8,128)(2,1)} %bitcast.138), calls=%async_computation.3 | async-start | bytes 2097152 | tf_op jit(solution)/shard_map/all_to_all | solution.py:268
  102.4 5.9 %fusion.47 = f32[1024,512]{1,0:T(8,128)S(1)} fusion(bf16[1024,2048]{1,0:T(8,128)(2,1)} %get-tuple-element.27, f32[1024,512]{1,0:T(8,128)} %get-tuple-element.30, f32[1024,512]{1,0:T(8,128)} %get-tuple-element.31), kind=kOutput, calls=%fused_computation.100 | convolution fusion | flops 2150629376 | bytes 10485760 | tf_op jit(solution)/shard_map/dot_general | solution.py:124
  108.4 2.3 fusion.46
  110.7 3.3 %add_convert_fusion.2 = bf16[1024,512]{1,0:T(8,128)(2,1)} fusion(f32[1024,512]{1,0:T(8,128)S(1)} %fusion.47, f32[1024,512]{1,0:T(8,128)S(1)} %fusion.46, bf16[1024,2048]{1,0:T(8,128)(2,1)S(1)} %copy-done.2, f32[1024,512]{1,0:T(8,128)S(1)} %copy-done.15, f32[1024,512]{1,0:T(8,128)S(1)} %copy-done.16), kind=kOutput, calls=%fused_computation.63 | convolution fusion | flops 2153250816 | bytes 13631488 | tf_op jit(solution)/shard_map/dot_general | solution.py:124
  114.1 13.7 %all-to-all-done.3 = bf16[8,128,512]{2,1,0:T(8,128)(2,1)} async-done(((bf16[8,128,512]{2,1,0:T(8,128)(2,1)}), bf16[8,128,512]{2,1,0:T(8,128)(2,1)}, u32[]{:S(2)}, u32[]{:S(2)}) %all-to-all-start.3) | async-done | bytes 1048608 | tf_op jit(solution)/shard_map/all_to_all | solution.py:268
  127.8 4.2 %all-to-all-start.1 = ((bf16[8,128,512]{2,1,0:T(8,128)(2,1)}), bf16[8,128,512]{2,1,0:T(8,128)(2,1)}, u32[]{:S(2)}, u32[]{:S(2)}) async-start(bf16[8,128,512]{2,1,0:T(8,128)(2,1)} %bitcast.134), calls=%async_computation.1 | async-start | bytes 2097152 | tf_op jit(solution)/shard_map/all_to_all | solution.py:268
  132.0 2.3 copy.26
  135.7 2.9 copy.28
  138.6 2.6 copy.27
  142.5 2.8 convert_bitcast_fusion
  145.3 2.9 copy.25
  148.2 9.2 %all-to-all-done.1 = bf16[8,128,512]{2,1,0:T(8,128)(2,1)} async-done(((bf16[8,128,512]{2,1,0:T(8,128)(2,1)}), bf16[8,128,512]{2,1,0:T(8,128)(2,1)}, u32[]{:S(2)}, u32[]{:S(2)}) %all-to-all-start.1) | async-done | bytes 1048608 | tf_op jit(solution)/shard_map/all_to_all | solution.py:268
  157.4 2.8 convert_bitcast_fusion.1
  160.2 2.9 copy.22
  163.2 2.6 multiply_reduce_fusion.2
  166.3 2.5 psum.22
  168.8 2.2 multiply_reduce_fusion
  171.0 2.5 all-reduce
  173.5 4.4 %multiply_convert_fusion = bf16[128,8,512]{2,0,1:T(8,128)(2,1)} fusion(f32[128,8,512]{2,0,1:T(8,128)} %copy.28, f32[128,8,512]{2,0,1:T(8,128)} %copy.27, f32[128]{0:T(128)S(1)} %broadcast_multiply_fusion.1, f32[8,512]{1,0:T(8,128)S(1)} %mul.340, f32[128]{0:T(128)S(1)} %add_rsqrt_fusion, bf16[8,128,512]{2,1,0:T(8,128)(2,1)} %all-to-all-done.3), kind=kLoop, calls=%fused_computation.55 | loop fusion | flops 4718592 | bytes 6308864 | tf_op jit(solution)/shard_map/convert_element_type | solution.py:297
  177.8 4.7 %all-to-all-start.4 = ((bf16[128,8,512]{2,0,1:T(8,128)(2,1)}), bf16[128,8,512]{2,0,1:T(8,128)(2,1)}, u32[]{:S(2)}, u32[]{:S(2)}) async-start(bf16[128,8,512]{2,0,1:T(8,128)(2,1)} %multiply_convert_fusion), calls=%async_computation.4 | async-start | bytes 2097152 | tf_op jit(solution)/shard_map/all_to_all | solution.py:265
  182.5 4.3 %fusion.16 = (bf16[128,4096]{0,1:T(8,128)(2,1)}, bf16[128,4096]{0,1:T(8,128)(2,1)}) fusion(f32[128,8,512]{0,2,1:T(8,128)} %copy.25, bf16[1,128,4096]{1,2,0:T(8,128)(2,1)} %copy.26, f32[128]{0:T(128)S(1)} %broadcast_multiply_fusion.1, f32[128]{0:T(128)S(1)} %add_rsqrt_fusion, f32[4096]{0:T(1024)S(1)} %bitcast.143, bf16[128,3,4096]{0,2,1:T(8,128)(2,1)S(1)} %bitcast.123, ...), kind=kLoop, calls=%fused_computation.48 | loop fusion | flops 7864320 | bytes 9455104 | tf_op jit(solution)/shard_map/convert_element_type | solution.py:298
  187.3 1.5 collective-permute-start.2
  188.8 20.0 %all-to-all-done.4 = bf16[128,8,512]{2,0,1:T(8,128)(2,1)} async-done(((bf16[128,8,512]{2,0,1:T(8,128)(2,1)}), bf16[128,8,512]{2,0,1:T(8,128)(2,1)}, u32[]{:S(2)}, u32[]{:S(2)}) %all-to-all-start.4) | async-done | bytes 1048608 | tf_op jit(solution)/shard_map/all_to_all | solution.py:265
  208.9 5.0 %fusion.73 = f32[2048,512]{1,0:T(8,128)S(1)} fusion(bf16[1024,2048]{1,0:T(8,128)(2,1)} %get-tuple-element.27, bf16[1024,512]{1,0:T(8,128)(2,1)} %bitcast.24), kind=kOutput, calls=%fused_computation.135 | convolution fusion | flops 2147483648 | bytes 9437184 | tf_op jit(solution)/shard_map/dot_general | solution.py:118
  213.9 3.9 %add_multiply_fusion = f32[2048,512]{1,0:T(8,128)S(1)} fusion(f32[2048,512]{1,0:T(8,128)S(1)} %fusion.73, bf16[1024,2048]{1,0:T(8,128)(2,1)S(1)} %copy-done.14, bf16[1024,512]{1,0:T(8,128)(2,1)} %bitcast.24, f32[2048]{0:T(1024)S(1)} %select_multiply_fusion), kind=kOutput, calls=%fused_computation.21 | convolution fusion | flops 2149580800 | bytes 13639680 | tf_op jit(solution)/shard_map/dot_general | solution.py:118
  217.9 2.6 add_select_fusion
  220.5 2.3 fusion.51
  222.8 2.3 fusion.50
  225.1 3.3 %add_convert_fusion = bf16[1024,512]{1,0:T(8,128)(2,1)} fusion(f32[1024,512]{1,0:T(8,128)S(1)} %fusion.51, f32[1024,512]{1,0:T(8,128)S(1)} %fusion.50, bf16[1024,2048]{1,0:T(8,128)(2,1)S(1)} %copy-done.3, f32[1024,512]{1,0:T(8,128)S(1)} %get-tuple-element.28, f32[1024,512]{1,0:T(8,128)S(1)} %get-tuple-element.29), kind=kOutput, calls=%fused_computation.53 | convolution fusion | flops 2153250816 | bytes 13631488 | tf_op jit(solution)/shard_map/dot_general | solution.py:124
  228.5 6.4 %collective-permute-done.2 = bf16[128,4096]{0,1:T(8,128)(2,1)} collective-permute-done((bf16[128,4096]{0,1:T(8,128)(2,1)}, bf16[128,4096]{0,1:T(8,128)(2,1)}, u32[]{:S(2)}, u32[]{:S(2)}) %collective-permute-start.2) | collective-permute-done | bytes 1048608 | tf_op jit(solution)/shard_map/ppermute | solution.py:19
  234.8 5.9 %all-to-all-start.5 = ((bf16[8,128,512]{2,1,0:T(8,128)(2,1)}), bf16[8,128,512]{2,1,0:T(8,128)(2,1)S(1)}, u32[]{:S(2)}, u32[]{:S(2)}) async-start(bf16[8,128,512]{2,1,0:T(8,128)(2,1)} %bitcast.135), calls=%async_computation.5 | async-start | bytes 2097152 | tf_op jit(solution)/shard_map/all_to_all | solution.py:268
  240.7 6.5 %fusion.53 = f32[512,1024]{1,0:T(8,128)} fusion(bf16[1024,2048]{1,0:T(8,128)(2,1)} %get-tuple-element.27, f32[1024,512]{1,0:T(8,128)} %get-tuple-element.19, f32[1024,512]{1,0:T(8,128)S(1)} %get-tuple-element.18), kind=kOutput, calls=%fused_computation.106 | convolution fusion | flops 2150629376 | bytes 10485760 | tf_op jit(solution)/shard_map/dot_general | solution.py:309
  247.2 18.6 %all-to-all-done.5 = bf16[8,128,512]{2,1,0:T(8,128)(2,1)S(1)} async-done(((bf16[8,128,512]{2,1,0:T(8,128)(2,1)}), bf16[8,128,512]{2,1,0:T(8,128)(2,1)S(1)}, u32[]{:S(2)}, u32[]{:S(2)}) %all-to-all-start.5) | async-done | bytes 1048608 | tf_op jit(solution)/shard_map/all_to_all | solution.py:268
  267.7 6.6 %fusion.52 = f32[512,1024]{1,0:T(8,128)} fusion(bf16[1024,2048]{1,0:T(8,128)(2,1)} %get-tuple-element.26, f32[1024,512]{1,0:T(8,128)} %get-tuple-element.19, f32[1024,512]{1,0:T(8,128)S(1)} %get-tuple-element.18), kind=kOutput, calls=%fused_computation.105 | convolution fusion | flops 2150629376 | bytes 10485760 | tf_op jit(solution)/shard_map/dot_general | solution.py:309
  274.3 2.3 copy.31
  276.5 7.8 %add_bitcast_fusion = f32[1,1,512,1024]{3,2,1,0:T(8,128)} fusion(f32[512,1024]{1,0:T(8,128)} %fusion.53, f32[512,1024]{1,0:T(8,128)} %fusion.52, bf16[1024,2048]{1,0:T(8,128)(2,1)} %get-tuple-element.27, f32[1024,512]{1,0:T(8,128)} %get-tuple-element.19, f32[1024,512]{1,0:T(8,128)S(1)} %get-tuple-element.18), kind=kOutput, calls=%fused_computation.51 | convolution fusion | flops 2152726528 | bytes 14680064 | tf_op jit(solution)/shard_map/dot_general | solution.py:309
  284.3 5.9 %collective-permute-done.3 = bf16[128,4096]{0,1:T(8,128)(2,1)S(1)} collective-permute-done((bf16[128,4096]{0,1:T(8,128)(2,1)}, bf16[128,4096]{0,1:T(8,128)(2,1)S(1)}, u32[]{:S(2)}, u32[]{:S(2)}) %collective-permute-start.3) | collective-permute-done | bytes 1048608 | tf_op jit(solution)/shard_map/ppermute | solution.py:19
  290.2 2.0 fusion.27
  292.2 1.6 maximum_bitcast_fusion
  293.8 2.8 copy.32
  (65 shorter events, 10.0 us)
Async XLA Ops:
  5.6 76.1 %collective-permute-start.1 = (bf16[128,2,4096]{0,2,1:T(8,128)(2,1)}, bf16[128,2,4096]{0,2,1:T(8,128)(2,1)}, u32[]{:S(2)}, u32[]{:S(2)}) collective-permute-start(bf16[128,2,4096]{0,2,1:T(8,128)(2,1)} %slice.90), channel_id=1, source_target_pairs={{0,16},{16,0},{1,17},{17,1},{2,18},{18,2},{3,19},{19,3},{4,20},{20... | collective-permute-start | bytes 6291464 | tf_op jit(solution)/shard_map/ppermute | solution.py:19
  9.8 31.6 %all-to-all-start.2 = ((bf16[128,8,512]{0,2,1:T(8,128)(2,1)}), bf16[128,8,512]{0,2,1:T(8,128)(2,1)}, u32[]{:S(2)}, u32[]{:S(2)}) async-start(bf16[128,8,512]{0,2,1:T(8,128)(2,1)} %bitcast.130), calls=%async_computation.2 | async-start | bytes 2097152 | tf_op jit(solution)/shard_map/all_to_all | solution.py:265
  25.8 3.4 %copy-start.8 = (f32[32,32,1024]{2,1,0:T(8,128)S(1)}, f32[32,32,1024]{2,1,0:T(8,128)}, u32[]{:S(2)}) copy-start(f32[32,32,1024]{2,1,0:T(8,128)} %get-tuple-element.34) | copy-start | bytes 12582916
  29.3 4.2 %copy-start.7 = (bf16[1,128,3,4096]{1,3,2,0:T(8,128)(2,1)S(1)}, bf16[1,128,3,4096]{1,3,2,0:T(8,128)(2,1)}, u32[]{:S(2)}) copy-start(bf16[1,128,3,4096]{1,3,2,0:T(8,128)(2,1)} %copy.20) | copy-start | bytes 9437188
  41.3 30.0 %all-to-all-start = ((bf16[128,8,512]{0,2,1:T(8,128)(2,1)}), bf16[128,8,512]{0,2,1:T(8,128)(2,1)}, u32[]{:S(2)}, u32[]{:S(2)}) async-start(bf16[128,8,512]{0,2,1:T(8,128)(2,1)} %bitcast.131), calls=%async_computation | async-start | bytes 2097152 | tf_op jit(solution)/shard_map/all_to_all | solution.py:265
  45.9 5.5 %copy-start.11 = (bf16[1024,2048]{1,0:T(8,128)(2,1)S(1)}, bf16[1024,2048]{1,0:T(8,128)(2,1)}, u32[]{:S(2)}) copy-start(bf16[1024,2048]{1,0:T(8,128)(2,1)} %get-tuple-element.26) | copy-start | bytes 12582916
  45.9 5.5 %copy-start.17 = (f32[1,1,512,1024]{3,2,1,0:T(8,128)S(1)}, f32[1,1,512,1024]{3,2,1,0:T(8,128)}, u32[]{:S(2)}) copy-start(f32[1,1,512,1024]{3,2,1,0:T(8,128)} %param.8) | copy-start | bytes 6291460
  51.4 2.4 copy-start
  74.1 5.1 %copy-start.12 = (bf16[1024,2048]{1,0:T(8,128)(2,1)S(1)}, bf16[1024,2048]{1,0:T(8,128)(2,1)}, u32[]{:S(2)}) copy-start(bf16[1024,2048]{1,0:T(8,128)(2,1)} %get-tuple-element.26) | copy-start | bytes 12582916
  74.1 5.1 %copy-start.20 = (bf16[8,128,512]{2,1,0:T(8,128)(2,1)S(1)}, bf16[8,128,512]{2,1,0:T(8,128)(2,1)}, u32[]{:S(2)}) copy-start(bf16[8,128,512]{2,1,0:T(8,128)(2,1)} %copy.21) | copy-start | bytes 3145732
  79.2 2.4 copy-start.19
  81.6 2.5 copy-start.1
  84.1 2.6 copy-start.5
  86.7 3.5 %copy-start.9 = (f32[2048,512]{1,0:T(8,128)}, f32[2048,512]{1,0:T(8,128)S(1)}, u32[]{:S(2)}) copy-start(f32[2048,512]{1,0:T(8,128)S(1)} %convolution_add_fusion) | copy-start | bytes 12582916
  98.1 29.6 %all-to-all-start.3 = ((bf16[8,128,512]{2,1,0:T(8,128)(2,1)}), bf16[8,128,512]{2,1,0:T(8,128)(2,1)}, u32[]{:S(2)}, u32[]{:S(2)}) async-start(bf16[8,128,512]{2,1,0:T(8,128)(2,1)} %bitcast.138), calls=%async_computation.3 | async-start | bytes 2097152 | tf_op jit(solution)/shard_map/all_to_all | solution.py:268
  102.4 6.0 %copy-start.13 = (bf16[1024,2048]{1,0:T(8,128)(2,1)S(1)}, bf16[1024,2048]{1,0:T(8,128)(2,1)}, u32[]{:S(2)}) copy-start(bf16[1024,2048]{1,0:T(8,128)(2,1)} %get-tuple-element.26) | copy-start | bytes 12582916
  102.4 6.0 %copy-start.15 = (f32[1024,512]{1,0:T(8,128)S(1)}, f32[1024,512]{1,0:T(8,128)}, u32[]{:S(2)}) copy-start(f32[1024,512]{1,0:T(8,128)} %get-tuple-element.30) | copy-start | bytes 6291460
  102.4 6.0 %copy-start.16 = (f32[1024,512]{1,0:T(8,128)S(1)}, f32[1024,512]{1,0:T(8,128)}, u32[]{:S(2)}) copy-start(f32[1024,512]{1,0:T(8,128)} %get-tuple-element.31) | copy-start | bytes 6291460
  108.4 2.4 copy-start.2
  127.8 29.6 %all-to-all-start.1 = ((bf16[8,128,512]{2,1,0:T(8,128)(2,1)}), bf16[8,128,512]{2,1,0:T(8,128)(2,1)}, u32[]{:S(2)}, u32[]{:S(2)}) async-start(bf16[8,128,512]{2,1,0:T(8,128)(2,1)} %bitcast.134), calls=%async_computation.1 | async-start | bytes 2097152 | tf_op jit(solution)/shard_map/all_to_all | solution.py:268
  138.6 3.2 %copy-start.21 = (f32[1,4096]{1,0:T(1,128)S(1)}, f32[1,4096]{1,0:T(1,128)}, u32[]{:S(2)}) copy-start(f32[1,4096]{1,0:T(1,128)} %param.9) | copy-start | bytes 49156
  163.2 2.6 copy-start.6
  177.8 31.0 %all-to-all-start.4 = ((bf16[128,8,512]{2,0,1:T(8,128)(2,1)}), bf16[128,8,512]{2,0,1:T(8,128)(2,1)}, u32[]{:S(2)}, u32[]{:S(2)}) async-start(bf16[128,8,512]{2,0,1:T(8,128)(2,1)} %multiply_convert_fusion), calls=%async_computation.4 | async-start | bytes 2097152 | tf_op jit(solution)/shard_map/all_to_all | solution.py:265
  186.8 41.7 %collective-permute-start = (bf16[128,4096]{0,1:T(8,128)(2,1)}, bf16[128,4096]{0,1:T(8,128)(2,1)S(1)}, u32[]{:S(2)}, u32[]{:S(2)}) collective-permute-start(bf16[128,4096]{0,1:T(8,128)(2,1)} %get-tuple-element.37), channel_id=1, source_target_pairs={{0,16},{16,0},{1,17},{17,1},{2,18},{18,2},{3,19},{19,3},{4,20},{20... | collective-permute-start | bytes 3145736 | tf_op jit(solution)/shard_map/ppermute | solution.py:19
  187.3 47.5 %collective-permute-start.2 = (bf16[128,4096]{0,1:T(8,128)(2,1)}, bf16[128,4096]{0,1:T(8,128)(2,1)}, u32[]{:S(2)}, u32[]{:S(2)}) collective-permute-start(bf16[128,4096]{0,1:T(8,128)(2,1)} %get-tuple-element.36), channel_id=1, source_target_pairs={{0,16},{16,0},{1,17},{17,1},{2,18},{18,2},{3,19},{19,3},{4,20},{20... | collective-permute-start | bytes 3145736 | tf_op jit(solution)/shard_map/ppermute | solution.py:19
  208.9 5.0 %copy-start.14 = (bf16[1024,2048]{1,0:T(8,128)(2,1)S(1)}, bf16[1024,2048]{1,0:T(8,128)(2,1)}, u32[]{:S(2)}) copy-start(bf16[1024,2048]{1,0:T(8,128)(2,1)} %get-tuple-element.26) | copy-start | bytes 12582916
  213.9 4.0 %copy-start.4 = (f32[2048,512]{1,0:T(8,128)S(1)}, f32[2048,512]{1,0:T(8,128)}, u32[]{:S(2)}) copy-start(f32[2048,512]{1,0:T(8,128)} %get-tuple-element.41) | copy-start | bytes 12582916
  213.9 4.0 %copy-start.10 = (f32[2048,512]{1,0:T(8,128)S(1)}, f32[2048,512]{1,0:T(8,128)}, u32[]{:S(2)}) copy-start(f32[2048,512]{1,0:T(8,128)} %copy-done.9) | copy-start | bytes 12582916
  217.9 2.6 copy-start.3
  228.4 6.4 %copy-start.18 = (bf16[128,4096]{0,1:T(8,128)(2,1)}, bf16[128,4096]{0,1:T(8,128)(2,1)S(1)}, u32[]{:S(2)}) copy-start(bf16[128,4096]{0,1:T(8,128)(2,1)S(1)} %collective-permute-done) | copy-start | bytes 3145732
  234.8 31.0 %all-to-all-start.5 = ((bf16[8,128,512]{2,1,0:T(8,128)(2,1)}), bf16[8,128,512]{2,1,0:T(8,128)(2,1)S(1)}, u32[]{:S(2)}, u32[]{:S(2)}) async-start(bf16[8,128,512]{2,1,0:T(8,128)(2,1)} %bitcast.135), calls=%async_computation.5 | async-start | bytes 2097152 | tf_op jit(solution)/shard_map/all_to_all | solution.py:268
  267.1 23.1 %collective-permute-start.3 = (bf16[128,4096]{0,1:T(8,128)(2,1)}, bf16[128,4096]{0,1:T(8,128)(2,1)S(1)}, u32[]{:S(2)}, u32[]{:S(2)}) collective-permute-start(bf16[128,4096]{0,1:T(8,128)(2,1)} %bitcast.139), channel_id=1, source_target_pairs={{0,16},{16,0},{1,17},{17,1},{2,18},{18,2},{3,19},{19,3},{4,20},{20... | collective-permute-start | bytes 3145736 | tf_op jit(solution)/shard_map/ppermute | solution.py:19

commit v2 on v1

--- a/solution.py
+++ b/solution.py
@@ -308,7 +308,8 @@
     dims = (((0,), (1,)), ((), ()))
     part = lambda a, b: lax.dot_general(a, b, dims, preferred_element_type=jnp.float32)
     filt_step = part(taps_hi, table_hi) + (part(taps_hi, table_lo) + part(taps_lo, table_hi))
-    sent_mix = from_partner(to_rows(grad_mix_cols), "pipe", 0).astype(jnp.float32)
+    grad_mix_rows, filt_step = lax.optimization_barrier((to_rows(grad_mix_cols), filt_step))
+    sent_mix = from_partner(grad_mix_rows, "pipe", 0).astype(jnp.float32)
     rest = jnp.stack(
         [
             sent_mix * partner_kv[:, 1].astype(jnp.float32),

time: 302 us -> 301 us (level)
  waiting for transfers between devices: 88.9 us -> 98.9 us
  matrix products: 84.3 us -> 75 us
    ppermute x4, waiting for transfers between devices: 12.3 us -> 27.4 us  [from_partner(): return lax.ppermute(block, axis, route)]
    dot_general x3, matrix products: 20.9 us -> 11.6 us  [on_device(): lax.dot_general(a, b, dims, preferred_element_type=jnp.float32)]
    all_to_all x3, waiting for transfers between devices: 41.4 us -> 36.2 us  [to_rows(): lax.all_to_all(columns, 'ctx', split_axis=0, concat_axis=1, tiled=True)]
    unnamed x50 -> x58, local copies, waits for them, and re-layouts: 16.6 us -> 15.7 us
  transfers between devices with their start and end apart: 10 -> 10, of which waited for: 8 -> 8; matrix products, arithmetic and copies ran while one was open for 41% -> 38% of each run, Pallas kernels for 0% -> 0%
where the time goes in v2:
time: 301 us; the launch traced here: 296 us
  waiting for transfers between devices  98.9 us (33%)
  matrix products  75 us (25%)
  other arithmetic  46.5 us (15%)
  starting transfers between devices  35 us (12%)
  local copies, waits for them, and re-layouts  34.2 us (11%)
  blocking collectives  4.93 us (2%)
    all_to_all x3, waiting for transfers between devices, to_rows(): lax.all_to_all(columns, 'ctx', split_axis=0, concat_axis=1, tiled=True)  36.2 us
    all_to_all x3, waiting for transfers between devices, to_columns(): return lax.all_to_all(rows, 'ctx', split_axis=1, concat_axis=0, tiled=True)  35.2 us
    dot_general x9, matrix products, dot_tt(): lax.dot_general(table, spec, (((1,), (0,)), ((), ())), preferred_element_...  27.5 us
    ppermute x4, waiting for transfers between devices, from_partner(): return lax.ppermute(block, axis, route)  27.4 us
    dot_general x6, matrix products, dot_tf(): lax.dot_general(table, signal, (((0,), (0,)), ((), ())), preferred_elemen...  21.4 us
    unnamed x58, local copies, waits for them, and re-layouts  15.7 us
    all_to_all x3, starting transfers between devices, to_columns(): return lax.all_to_all(rows, 'ctx', split_axis=1, concat_axis=0, tiled=True)  15 us
    dot_general x3, matrix products, dense_taps_spectrum(): lax.dot_general(a, b, dims, preferred_element_type=jnp.float32)  14.4 us
  transfers between devices with their start and end apart: 10, of which 8 were waited for; matrix products, arithmetic and copies ran while one was open for 38% of the time, Pallas kernels for 0%

profile of v2, /device:TPU:0, one launch (start us, length us, event | category | flops | bytes accessed | tf_op | source)
XLA Modules:
  0.0 295.9 jit_solution(14040234290621121848)
XLA Ops:
  0.6 3.5 %copy.23 = bf16[1,128,3,4096]{1,3,2,0:T(8,128)(2,1)S(1)} copy(bf16[1,128,3,4096]{3,1,2,0:T(8,128)(2,1)} %param.6) | data formatting | bytes 6291456 | tf_op args[1]
  4.1 1.5 slice.90
  5.6 2.9 collective-permute-start.1
  9.8 5.8 %all-to-all-start.2 = ((bf16[128,8,512]{0,2,1:T(8,128)(2,1)}), bf16[128,8,512]{0,2,1:T(8,128)(2,1)}, u32[]{:S(2)}, u32[]{:S(2)}) async-start(bf16[128,8,512]{0,2,1:T(8,128)(2,1)} %bitcast.129), calls=%async_computation.2 | async-start | bytes 2097152 | tf_op jit(solution)/shard_map/all_to_all | solution.py:265
  16.7 4.5 %multiply_subtract_fusion = (f32[32,32,1024]{2,1,0:T(8,128)}, f32[32,32,1024]{2,1,0:T(8,128)}) fusion(f32[32,1024]{1,0:T(8,128)S(1)} %get-tuple-element.46, f32[32,1024]{1,0:T(8,128)S(1)} %get-tuple-element.43, f32[32,1024]{1,0:T(8,128)S(1)} %get-tuple-element.47, f32[32,1024]{1,0:T(8,128)S(1)} %get-tuple-element.42), kind=kLoop, calls=%fused_computation.25 | loop fusion | flops 7340032 | bytes 8912896 | tf_op jit(solution)/shard_map/sub | solution.py:103
  21.2 4.6 %copy.20 = bf16[1,128,3,4096]{1,3,2,0:T(8,128)(2,1)} copy(bf16[1,128,3,4096]{3,1,2,0:T(8,128)(2,1)} %param.5) | data formatting | bytes 6291456 | tf_op args[0]
  25.9 2.8 bitcast_select_fusion
  29.3 4.2 %fusion = (bf16[1024,2048]{1,0:T(8,128)(2,1)}, bf16[1024,2048]{1,0:T(8,128)(2,1)}) fusion(f32[1024,1024]{1,0:T(8,128)S(1)} %bitcast_select_fusion, f32[1024,1024]{1,0:T(8,128)S(1)} %bitcast.127), kind=kLoop, calls=%fused_computation.2 | loop fusion | flops 10485760 | bytes 16777216 | tf_op jit(solution)/shard_map/convert_element_type | solution.py:85
  34.8 6.5 %all-to-all-done.2 = bf16[128,8,512]{0,2,1:T(8,128)(2,1)} async-done(((bf16[128,8,512]{0,2,1:T(8,128)(2,1)}), bf16[128,8,512]{0,2,1:T(8,128)(2,1)}, u32[]{:S(2)}, u32[]{:S(2)}) %all-to-all-start.2) | async-done | bytes 1048608 | tf_op jit(solution)/shard_map/all_to_all | solution.py:265
  41.3 4.5 %all-to-all-start = ((bf16[128,8,512]{0,2,1:T(8,128)(2,1)}), bf16[128,8,512]{0,2,1:T(8,128)(2,1)}, u32[]{:S(2)}, u32[]{:S(2)}) async-start(bf16[128,8,512]{0,2,1:T(8,128)(2,1)} %bitcast.130), calls=%async_computation | async-start | bytes 2097152 | tf_op jit(solution)/shard_map/all_to_all | solution.py:265
  45.9 5.5 %fusion.29 = f32[2048,512]{1,0:T(8,128)S(1)} fusion(bf16[1024,2048]{1,0:T(8,128)(2,1)} %get-tuple-element.31, f32[1,1,512,1024]{3,2,1,0:T(8,128)} %param.8), kind=kOutput, calls=%fused_computation.76 | convolution fusion | flops 2148532224 | bytes 10485760 | tf_op jit(solution)/shard_map/dot_general | solution.py:144
  51.4 2.4 fusion.28
  53.8 6.6 %broadcast_multiply_fusion = (f32[2048,512]{1,0:T(8,128)}, f32[2048,512]{1,0:T(8,128)}) fusion(f32[2048]{0:T(1024)S(1)} %select_multiply_fusion, f32[2048,512]{1,0:T(8,128)S(1)} %fusion.29, f32[2048,512]{1,0:T(8,128)S(1)} %fusion.28, bf16[1024,2048]{1,0:T(8,128)(2,1)S(1)} %copy-done, f32[1,1,512,1024]{3,2,1,0:T(8,128)S(1)} %copy-done.20), kind=kOutput, calls=%fused_computation.65 | convolution fusion | flops 2152202240 | bytes 23076864 | tf_op jit(solution)/shard_map/dot_general | solution.py:144
  60.4 2.3 copy.24
  62.7 8.7 %all-to-all-done = bf16[128,8,512]{0,2,1:T(8,128)(2,1)} async-done(((bf16[128,8,512]{0,2,1:T(8,128)(2,1)}), bf16[128,8,512]{0,2,1:T(8,128)(2,1)}, u32[]{:S(2)}, u32[]{:S(2)}) %all-to-all-start) | async-done | bytes 1048608 | tf_op jit(solution)/shard_map/all_to_all | solution.py:265
  71.3 2.7 copy.21
  74.1 5.1 %fusion.71 = f32[2048,512]{1,0:T(8,128)S(1)} fusion(bf16[1024,2048]{1,0:T(8,128)(2,1)} %get-tuple-element.31, bf16[1024,512]{1,0:T(8,128)(2,1)} %bitcast.139), kind=kOutput, calls=%fused_computation.133 | convolution fusion | flops 2147483648 | bytes 9437184 | tf_op jit(solution)/shard_map/dot_general | solution.py:118
  79.2 2.4 convolution_add_fusion.1
  81.6 2.4 fusion.72
  84.1 2.5 convolution_add_fusion
  86.7 3.4 %subtract_select_fusion = (f32[1024,512]{1,0:T(8,128)S(1)}, f32[1024,512]{1,0:T(8,128)S(1)}, f32[1024,512]{1,0:T(8,128)}, f32[1024,512]{1,0:T(8,128)}) fusion(f32[2048,512]{1,0:T(8,128)S(1)} %convolution_add_fusion, f32[2048,512]{1,0:T(8,128)S(1)} %copy-done.6, pred[1024]{0:T(1024)(128)(4,1)S(1)} %get-tuple-element.50, f32[2048,512]{1,0:T(8,128)S(1)} %convolution_add_fusion.1), kind=kLoop, calls=%fused_computation.29 | loop fusion | flops 8388608 | bytes 20972544 | tf_op jit(solution)/shard_map/jit(_where)/select_n | solution.py:165
  90.1 2.3 fusion.49
  92.4 2.3 fusion.48
  94.8 3.3 %add_convert_fusion.1 = bf16[1024,512]{1,0:T(8,128)(2,1)} fusion(f32[1024,512]{1,0:T(8,128)S(1)} %fusion.49, f32[1024,512]{1,0:T(8,128)S(1)} %fusion.48, bf16[1024,2048]{1,0:T(8,128)(2,1)S(1)} %copy-done.1, f32[1024,512]{1,0:T(8,128)S(1)} %get-tuple-element.27, f32[1024,512]{1,0:T(8,128)S(1)} %get-tuple-element.26), kind=kOutput, calls=%fused_computation.58 | convolution fusion | flops 2153250816 | bytes 13631488 | tf_op jit(solution)/shard_map/dot_general | solution.py:124
  98.1 4.2 %all-to-all-start.3 = ((bf16[8,128,512]{2,1,0:T(8,128)(2,1)}), bf16[8,128,512]{2,1,0:T(8,128)(2,1)}, u32[]{:S(2)}, u32[]{:S(2)}) async-start(bf16[8,128,512]{2,1,0:T(8,128)(2,1)} %bitcast.137), calls=%async_computation.3 | async-start | bytes 2097152 | tf_op jit(solution)/shard_map/all_to_all | solution.py:268
  102.4 5.9 %fusion.47 = f32[1024,512]{1,0:T(8,128)S(1)} fusion(bf16[1024,2048]{1,0:T(8,128)(2,1)} %get-tuple-element.31, f32[1024,512]{1,0:T(8,128)} %get-tuple-element.34, f32[1024,512]{1,0:T(8,128)} %get-tuple-element.35), kind=kOutput, calls=%fused_computation.100 | convolution fusion | flops 2150629376 | bytes 10485760 | tf_op jit(solution)/shard_map/dot_general | solution.py:124
  108.3 2.3 fusion.46
  110.7 3.3 %add_convert_fusion.2 = bf16[1024,512]{1,0:T(8,128)(2,1)} fusion(f32[1024,512]{1,0:T(8,128)S(1)} %fusion.47, f32[1024,512]{1,0:T(8,128)S(1)} %fusion.46, bf16[1024,2048]{1,0:T(8,128)(2,1)S(1)} %copy-done.2, f32[1024,512]{1,0:T(8,128)S(1)} %copy-done.18, f32[1024,512]{1,0:T(8,128)S(1)} %copy-done.19), kind=kOutput, calls=%fused_computation.63 | convolution fusion | flops 2153250816 | bytes 13631488 | tf_op jit(solution)/shard_map/dot_general | solution.py:124
  114.0 13.7 %all-to-all-done.3 = bf16[8,128,512]{2,1,0:T(8,128)(2,1)} async-done(((bf16[8,128,512]{2,1,0:T(8,128)(2,1)}), bf16[8,128,512]{2,1,0:T(8,128)(2,1)}, u32[]{:S(2)}, u32[]{:S(2)}) %all-to-all-start.3) | async-done | bytes 1048608 | tf_op jit(solution)/shard_map/all_to_all | solution.py:268
  127.7 4.2 %all-to-all-start.1 = ((bf16[8,128,512]{2,1,0:T(8,128)(2,1)}), bf16[8,128,512]{2,1,0:T(8,128)(2,1)}, u32[]{:S(2)}, u32[]{:S(2)}) async-start(bf16[8,128,512]{2,1,0:T(8,128)(2,1)} %bitcast.133), calls=%async_computation.1 | async-start | bytes 2097152 | tf_op jit(solution)/shard_map/all_to_all | solution.py:268
  132.0 2.3 copy.26
  134.3 1.5 slice_convert_fusion
  135.7 3.0 %copy.28 = f32[128,8,512]{2,0,1:T(8,128)} copy(f32[128,8,512]{0,2,1:T(8,128)} %bitcast.128) | data formatting | bytes 4194304 | tf_op jit(solution)/shard_map/convert_element_type | solution.py:289
  138.7 2.6 copy.27
  142.6 2.8 convert_bitcast_fusion
  145.4 2.9 copy.25
  148.3 9.1 %all-to-all-done.1 = bf16[8,128,512]{2,1,0:T(8,128)(2,1)} async-done(((bf16[8,128,512]{2,1,0:T(8,128)(2,1)}), bf16[8,128,512]{2,1,0:T(8,128)(2,1)}, u32[]{:S(2)}, u32[]{:S(2)}) %all-to-all-start.1) | async-done | bytes 1048608 | tf_op jit(solution)/shard_map/all_to_all | solution.py:268
  157.4 2.8 convert_bitcast_fusion.1
  160.2 2.9 copy.22
  163.1 2.6 multiply_reduce_fusion.2
  166.2 2.5 psum.22
  168.7 2.2 multiply_reduce_fusion
  170.9 2.5 all-reduce
  173.4 4.3 %multiply_convert_fusion = bf16[128,8,512]{2,0,1:T(8,128)(2,1)} fusion(f32[128,8,512]{2,0,1:T(8,128)} %copy.28, f32[128,8,512]{2,0,1:T(8,128)} %copy.27, f32[128]{0:T(128)S(1)} %broadcast_multiply_fusion.1, f32[8,512]{1,0:T(8,128)S(1)} %mul.340, f32[128]{0:T(128)S(1)} %add_rsqrt_fusion, bf16[8,128,512]{2,1,0:T(8,128)(2,1)} %all-to-all-done.3), kind=kLoop, calls=%fused_computation.55 | loop fusion | flops 4718592 | bytes 6308864 | tf_op jit(solution)/shard_map/convert_element_type | solution.py:297
  177.7 4.7 %all-to-all-start.4 = ((bf16[128,8,512]{2,0,1:T(8,128)(2,1)}), bf16[128,8,512]{2,0,1:T(8,128)(2,1)}, u32[]{:S(2)}, u32[]{:S(2)}) async-start(bf16[128,8,512]{2,0,1:T(8,128)(2,1)} %multiply_convert_fusion), calls=%async_computation.4 | async-start | bytes 2097152 | tf_op jit(solution)/shard_map/all_to_all | solution.py:265
  182.4 4.3 %fusion.16 = (bf16[128,4096]{0,1:T(8,128)(2,1)}, bf16[128,4096]{0,1:T(8,128)(2,1)}) fusion(f32[128,8,512]{0,2,1:T(8,128)} %copy.25, bf16[1,128,4096]{1,2,0:T(8,128)(2,1)} %copy.26, f32[128]{0:T(128)S(1)} %broadcast_multiply_fusion.1, f32[128]{0:T(128)S(1)} %add_rsqrt_fusion, f32[4096]{0:T(1024)S(1)} %bitcast.142, bf16[128,3,4096]{0,2,1:T(8,128)(2,1)S(1)} %bitcast.122, ...), kind=kLoop, calls=%fused_computation.48 | loop fusion | flops 7864320 | bytes 9455104 | tf_op jit(solution)/shard_map/convert_element_type | solution.py:298
  187.2 1.5 collective-permute-start.2
  188.7 20.0 %all-to-all-done.4 = bf16[128,8,512]{2,0,1:T(8,128)(2,1)} async-done(((bf16[128,8,512]{2,0,1:T(8,128)(2,1)}), bf16[128,8,512]{2,0,1:T(8,128)(2,1)}, u32[]{:S(2)}, u32[]{:S(2)}) %all-to-all-start.4) | async-done | bytes 1048608 | tf_op jit(solution)/shard_map/all_to_all | solution.py:265
  208.8 5.0 %fusion.73 = f32[2048,512]{1,0:T(8,128)S(1)} fusion(bf16[1024,2048]{1,0:T(8,128)(2,1)} %get-tuple-element.31, bf16[1024,512]{1,0:T(8,128)(2,1)} %bitcast.24), kind=kOutput, calls=%fused_computation.135 | convolution fusion | flops 2147483648 | bytes 9437184 | tf_op jit(solution)/shard_map/dot_general | solution.py:118
  213.8 3.9 %add_multiply_fusion = f32[2048,512]{1,0:T(8,128)S(1)} fusion(f32[2048,512]{1,0:T(8,128)S(1)} %fusion.73, bf16[1024,2048]{1,0:T(8,128)(2,1)S(1)} %copy-done.15, bf16[1024,512]{1,0:T(8,128)(2,1)} %bitcast.24, f32[2048]{0:T(1024)S(1)} %select_multiply_fusion), kind=kOutput, calls=%fused_computation.21 | convolution fusion | flops 2149580800 | bytes 13639680 | tf_op jit(solution)/shard_map/dot_general | solution.py:118
  217.8 2.6 add_select_fusion
  220.4 2.3 fusion.51
  222.7 2.3 fusion.50
  225.0 3.3 %add_convert_fusion = bf16[1024,512]{1,0:T(8,128)(2,1)} fusion(f32[1024,512]{1,0:T(8,128)S(1)} %fusion.51, f32[1024,512]{1,0:T(8,128)S(1)} %fusion.50, bf16[1024,2048]{1,0:T(8,128)(2,1)S(1)} %copy-done.3, f32[1024,512]{1,0:T(8,128)S(1)} %get-tuple-element.32, f32[1024,512]{1,0:T(8,128)S(1)} %get-tuple-element.33), kind=kOutput, calls=%fused_computation.53 | convolution fusion | flops 2153250816 | bytes 13631488 | tf_op jit(solution)/shard_map/dot_general | solution.py:124
  228.3 6.4 %collective-permute-done.2 = bf16[128,4096]{0,1:T(8,128)(2,1)} collective-permute-done((bf16[128,4096]{0,1:T(8,128)(2,1)}, bf16[128,4096]{0,1:T(8,128)(2,1)}, u32[]{:S(2)}, u32[]{:S(2)}) %collective-permute-start.2) | collective-permute-done | bytes 1048608 | tf_op jit(solution)/shard_map/ppermute | solution.py:19
  234.7 5.9 %all-to-all-start.5 = ((bf16[8,128,512]{2,1,0:T(8,128)(2,1)}), bf16[8,128,512]{2,1,0:T(8,128)(2,1)S(1)}, u32[]{:S(2)}, u32[]{:S(2)}) async-start(bf16[8,128,512]{2,1,0:T(8,128)(2,1)} %bitcast.134), calls=%async_computation.5 | async-start | bytes 2097152 | tf_op jit(solution)/shard_map/all_to_all | solution.py:268
  240.6 5.4 %fusion.53 = f32[512,1024]{1,0:T(8,128)S(1)} fusion(bf16[1024,2048]{1,0:T(8,128)(2,1)} %get-tuple-element.31, f32[1024,512]{1,0:T(8,128)} %get-tuple-element.23, f32[1024,512]{1,0:T(8,128)S(1)} %get-tuple-element.22), kind=kOutput, calls=%fused_computation.106 | convolution fusion | flops 2150629376 | bytes 10485760 | tf_op jit(solution)/shard_map/dot_general | solution.py:309
  246.0 2.5 fusion.52
  248.5 3.8 %add_add_fusion.1 = f32[512,1024]{1,0:T(8,128)} fusion(f32[512,1024]{1,0:T(8,128)S(1)} %fusion.53, f32[512,1024]{1,0:T(8,128)S(1)} %fusion.52, bf16[1024,2048]{1,0:T(8,128)(2,1)S(1)} %copy-done.4, f32[1024,512]{1,0:T(8,128)S(1)} %copy-done.17, f32[1024,512]{1,0:T(8,128)S(1)} %get-tuple-element.22), kind=kOutput, calls=%fused_computation.51 | convolution fusion | flops 2152726528 | bytes 14680064 | tf_op jit(solution)/shard_map/dot_general | solution.py:309
  252.3 13.4 %all-to-all-done.5 = bf16[8,128,512]{2,1,0:T(8,128)(2,1)S(1)} async-done(((bf16[8,128,512]{2,1,0:T(8,128)(2,1)}), bf16[8,128,512]{2,1,0:T(8,128)(2,1)S(1)}, u32[]{:S(2)}, u32[]{:S(2)}) %all-to-all-start.5) | async-done | bytes 1048608 | tf_op jit(solution)/shard_map/all_to_all | solution.py:268
  268.3 21.0 %collective-permute-done.3 = bf16[128,4096]{0,1:T(8,128)(2,1)S(1)} collective-permute-done((bf16[128,4096]{0,1:T(8,128)(2,1)S(1)}, bf16[128,4096]{0,1:T(8,128)(2,1)S(1)}, u32[]{:S(2)}, u32[]{:S(2)}) %collective-permute-start.3) | collective-permute-done | bytes 1048608 | tf_op jit(solution)/shard_map/ppermute | solution.py:19
  289.3 2.0 fusion.27
  291.3 1.6 maximum_bitcast_fusion
  292.9 2.8 copy.32
  (73 shorter events, 9.2 us)
Async XLA Ops:
  5.6 76.0 %collective-permute-start.1 = (bf16[128,2,4096]{0,2,1:T(8,128)(2,1)}, bf16[128,2,4096]{0,2,1:T(8,128)(2,1)}, u32[]{:S(2)}, u32[]{:S(2)}) collective-permute-start(bf16[128,2,4096]{0,2,1:T(8,128)(2,1)} %slice.90), channel_id=1, source_target_pairs={{0,16},{16,0},{1,17},{17,1},{2,18},{18,2},{3,19},{19,3},{4,20},{20... | collective-permute-start | bytes 6291464 | tf_op jit(solution)/shard_map/ppermute | solution.py:19
  9.8 31.6 %all-to-all-start.2 = ((bf16[128,8,512]{0,2,1:T(8,128)(2,1)}), bf16[128,8,512]{0,2,1:T(8,128)(2,1)}, u32[]{:S(2)}, u32[]{:S(2)}) async-start(bf16[128,8,512]{0,2,1:T(8,128)(2,1)} %bitcast.129), calls=%async_computation.2 | async-start | bytes 2097152 | tf_op jit(solution)/shard_map/all_to_all | solution.py:265
  25.9 3.4 %copy-start.9 = (f32[32,32,1024]{2,1,0:T(8,128)S(1)}, f32[32,32,1024]{2,1,0:T(8,128)}, u32[]{:S(2)}) copy-start(f32[32,32,1024]{2,1,0:T(8,128)} %get-tuple-element.38) | copy-start | bytes 12582916
  29.3 4.2 %copy-start.8 = (bf16[1,128,3,4096]{1,3,2,0:T(8,128)(2,1)S(1)}, bf16[1,128,3,4096]{1,3,2,0:T(8,128)(2,1)}, u32[]{:S(2)}) copy-start(bf16[1,128,3,4096]{1,3,2,0:T(8,128)(2,1)} %copy.20) | copy-start | bytes 9437188
  41.3 30.0 %all-to-all-start = ((bf16[128,8,512]{0,2,1:T(8,128)(2,1)}), bf16[128,8,512]{0,2,1:T(8,128)(2,1)}, u32[]{:S(2)}, u32[]{:S(2)}) async-start(bf16[128,8,512]{0,2,1:T(8,128)(2,1)} %bitcast.130), calls=%async_computation | async-start | bytes 2097152 | tf_op jit(solution)/shard_map/all_to_all | solution.py:265
  45.9 5.5 %copy-start.12 = (bf16[1024,2048]{1,0:T(8,128)(2,1)S(1)}, bf16[1024,2048]{1,0:T(8,128)(2,1)}, u32[]{:S(2)}) copy-start(bf16[1024,2048]{1,0:T(8,128)(2,1)} %get-tuple-element.30) | copy-start | bytes 12582916
  45.9 5.5 %copy-start.20 = (f32[1,1,512,1024]{3,2,1,0:T(8,128)S(1)}, f32[1,1,512,1024]{3,2,1,0:T(8,128)}, u32[]{:S(2)}) copy-start(f32[1,1,512,1024]{3,2,1,0:T(8,128)} %param.8) | copy-start | bytes 6291460
  51.4 2.4 copy-start
  74.1 5.1 %copy-start.13 = (bf16[1024,2048]{1,0:T(8,128)(2,1)S(1)}, bf16[1024,2048]{1,0:T(8,128)(2,1)}, u32[]{:S(2)}) copy-start(bf16[1024,2048]{1,0:T(8,128)(2,1)} %get-tuple-element.30) | copy-start | bytes 12582916
  74.1 5.1 %copy-start.24 = (bf16[8,128,512]{2,1,0:T(8,128)(2,1)S(1)}, bf16[8,128,512]{2,1,0:T(8,128)(2,1)}, u32[]{:S(2)}) copy-start(bf16[8,128,512]{2,1,0:T(8,128)(2,1)} %copy.21) | copy-start | bytes 3145732
  79.2 2.4 copy-start.23
  81.6 2.5 copy-start.1
  84.1 2.6 copy-start.6
  86.6 3.4 %copy-start.10 = (f32[2048,512]{1,0:T(8,128)}, f32[2048,512]{1,0:T(8,128)S(1)}, u32[]{:S(2)}) copy-start(f32[2048,512]{1,0:T(8,128)S(1)} %convolution_add_fusion) | copy-start | bytes 12582916
  98.1 29.7 %all-to-all-start.3 = ((bf16[8,128,512]{2,1,0:T(8,128)(2,1)}), bf16[8,128,512]{2,1,0:T(8,128)(2,1)}, u32[]{:S(2)}, u32[]{:S(2)}) async-start(bf16[8,128,512]{2,1,0:T(8,128)(2,1)} %bitcast.137), calls=%async_computation.3 | async-start | bytes 2097152 | tf_op jit(solution)/shard_map/all_to_all | solution.py:268
  102.3 6.0 %copy-start.14 = (bf16[1024,2048]{1,0:T(8,128)(2,1)S(1)}, bf16[1024,2048]{1,0:T(8,128)(2,1)}, u32[]{:S(2)}) copy-start(bf16[1024,2048]{1,0:T(8,128)(2,1)} %get-tuple-element.30) | copy-start | bytes 12582916
  102.3 6.0 %copy-start.18 = (f32[1024,512]{1,0:T(8,128)S(1)}, f32[1024,512]{1,0:T(8,128)}, u32[]{:S(2)}) copy-start(f32[1024,512]{1,0:T(8,128)} %get-tuple-element.34) | copy-start | bytes 6291460
  102.4 6.0 %copy-start.19 = (f32[1024,512]{1,0:T(8,128)S(1)}, f32[1024,512]{1,0:T(8,128)}, u32[]{:S(2)}) copy-start(f32[1024,512]{1,0:T(8,128)} %get-tuple-element.35) | copy-start | bytes 6291460
  108.3 2.4 copy-start.2
  127.7 29.6 %all-to-all-start.1 = ((bf16[8,128,512]{2,1,0:T(8,128)(2,1)}), bf16[8,128,512]{2,1,0:T(8,128)(2,1)}, u32[]{:S(2)}, u32[]{:S(2)}) async-start(bf16[8,128,512]{2,1,0:T(8,128)(2,1)} %bitcast.133), calls=%async_computation.1 | async-start | bytes 2097152 | tf_op jit(solution)/shard_map/all_to_all | solution.py:268
  138.7 3.2 %copy-start.25 = (f32[1,4096]{1,0:T(1,128)S(1)}, f32[1,4096]{1,0:T(1,128)}, u32[]{:S(2)}) copy-start(f32[1,4096]{1,0:T(1,128)} %param.9) | copy-start | bytes 49156
  163.1 2.6 copy-start.7
  177.7 31.0 %all-to-all-start.4 = ((bf16[128,8,512]{2,0,1:T(8,128)(2,1)}), bf16[128,8,512]{2,0,1:T(8,128)(2,1)}, u32[]{:S(2)}, u32[]{:S(2)}) async-start(bf16[128,8,512]{2,0,1:T(8,128)(2,1)} %multiply_convert_fusion), calls=%async_computation.4 | async-start | bytes 2097152 | tf_op jit(solution)/shard_map/all_to_all | solution.py:265
  186.7 41.6 %collective-permute-start = (bf16[128,4096]{0,1:T(8,128)(2,1)}, bf16[128,4096]{0,1:T(8,128)(2,1)S(1)}, u32[]{:S(2)}, u32[]{:S(2)}) collective-permute-start(bf16[128,4096]{0,1:T(8,128)(2,1)} %get-tuple-element.41), channel_id=1, source_target_pairs={{0,16},{16,0},{1,17},{17,1},{2,18},{18,2},{3,19},{19,3},{4,20},{20... | collective-permute-start | bytes 3145736 | tf_op jit(solution)/shard_map/ppermute | solution.py:19
  187.2 47.5 %collective-permute-start.2 = (bf16[128,4096]{0,1:T(8,128)(2,1)}, bf16[128,4096]{0,1:T(8,128)(2,1)}, u32[]{:S(2)}, u32[]{:S(2)}) collective-permute-start(bf16[128,4096]{0,1:T(8,128)(2,1)} %get-tuple-element.40), channel_id=1, source_target_pairs={{0,16},{16,0},{1,17},{17,1},{2,18},{18,2},{3,19},{19,3},{4,20},{20... | collective-permute-start | bytes 3145736 | tf_op jit(solution)/shard_map/ppermute | solution.py:19
  208.8 5.0 %copy-start.15 = (bf16[1024,2048]{1,0:T(8,128)(2,1)S(1)}, bf16[1024,2048]{1,0:T(8,128)(2,1)}, u32[]{:S(2)}) copy-start(bf16[1024,2048]{1,0:T(8,128)(2,1)} %get-tuple-element.30) | copy-start | bytes 12582916
  213.8 4.0 %copy-start.5 = (f32[2048,512]{1,0:T(8,128)S(1)}, f32[2048,512]{1,0:T(8,128)}, u32[]{:S(2)}) copy-start(f32[2048,512]{1,0:T(8,128)} %get-tuple-element.45) | copy-start | bytes 12582916
  213.8 4.0 %copy-start.11 = (f32[2048,512]{1,0:T(8,128)S(1)}, f32[2048,512]{1,0:T(8,128)}, u32[]{:S(2)}) copy-start(f32[2048,512]{1,0:T(8,128)} %copy-done.10) | copy-start | bytes 12582916
  217.8 2.6 copy-start.3
  228.3 6.4 %copy-start.21 = (bf16[128,4096]{0,1:T(8,128)(2,1)}, bf16[128,4096]{0,1:T(8,128)(2,1)S(1)}, u32[]{:S(2)}) copy-start(bf16[128,4096]{0,1:T(8,128)(2,1)S(1)} %collective-permute-done) | copy-start | bytes 3145732
  234.7 31.0 %all-to-all-start.5 = ((bf16[8,128,512]{2,1,0:T(8,128)(2,1)}), bf16[8,128,512]{2,1,0:T(8,128)(2,1)S(1)}, u32[]{:S(2)}, u32[]{:S(2)}) async-start(bf16[8,128,512]{2,1,0:T(8,128)(2,1)} %bitcast.134), calls=%async_computation.5 | async-start | bytes 2097152 | tf_op jit(solution)/shard_map/all_to_all | solution.py:268
  240.6 5.4 %copy-start.16 = (bf16[1024,2048]{1,0:T(8,128)(2,1)S(1)}, bf16[1024,2048]{1,0:T(8,128)(2,1)}, u32[]{:S(2)}) copy-start(bf16[1024,2048]{1,0:T(8,128)(2,1)} %get-tuple-element.30) | copy-start | bytes 12582916
  240.6 5.4 %copy-start.17 = (f32[1024,512]{1,0:T(8,128)S(1)}, f32[1024,512]{1,0:T(8,128)}, u32[]{:S(2)}) copy-start(f32[1024,512]{1,0:T(8,128)} %get-tuple-element.23) | copy-start | bytes 6291460
  246.0 2.5 copy-start.4
  252.3 14.7 %copy-start.22 = (bf16[128,4096]{0,1:T(8,128)(2,1)S(1)}, bf16[128,4096]{0,1:T(8,128)(2,1)}, u32[]{:S(2)}) copy-start(bf16[128,4096]{0,1:T(8,128)(2,1)} %copy-done.21) | copy-start | bytes 3145732
  266.4 22.9 %collective-permute-start.3 = (bf16[128,4096]{0,1:T(8,128)(2,1)S(1)}, bf16[128,4096]{0,1:T(8,128)(2,1)S(1)}, u32[]{:S(2)}, u32[]{:S(2)}) collective-permute-start(bf16[128,4096]{0,1:T(8,128)(2,1)S(1)} %bitcast.138), channel_id=1, source_target_pairs={{0,16},{16,0},{1,17},{17,1},{2,18},{18,2},{3,19},{19,3},{4,20},{20... | collective-permute-start | bytes 3145736 | tf_op jit(solution)/shard_map/ppermute | solution.py:19

commit v3 on v1

--- a/solution.py
+++ b/solution.py
@@ -298,17 +298,26 @@
     sent_first = from_partner((grad_y * conv_value).astype(jnp.bfloat16), "pipe", 0)
     grad_cols = to_columns(grad_z)
     grad_spec = dense_spectrum_exact(grad_cols, table) * weights
-    grad_mix_cols = dense_signal(dense_multiply(grad_spec, tap_spec, True), table).astype(
-        jnp.bfloat16
-    )
-    sent_rows, sent_first, grad_mix_cols = lax.optimization_barrier((sent_rows, sent_first, grad_mix_cols))
+    mix_prod = dense_multiply(grad_spec, tap_spec, True)
+    width = mix_prod.shape[1] // 2 if mix_prod.shape[1] % 256 == 0 else mix_prod.shape[1]
+    pieces = mix_prod.shape[1] // width
+    first_cols = dense_signal(mix_prod[:, :width], table).astype(jnp.bfloat16)
+    sent_rows, sent_first, first_cols = lax.optimization_barrier((sent_rows, sent_first, first_cols))
+    sent_parts = [from_partner(to_rows(first_cols), "pipe", 0)]
+    for piece in range(1, pieces):
+        piece_cols = dense_signal(mix_prod[:, piece * width : (piece + 1) * width], table)
+        sent_parts.append(from_partner(to_rows(piece_cols.astype(jnp.bfloat16)), "pipe", 0))
     taps_prod = dense_multiply(grad_spec, backward_spec, True)
     taps_hi, taps_lo = split_bf16(taps_prod)
     table_hi, table_lo = table
     dims = (((0,), (1,)), ((), ()))
     part = lambda a, b: lax.dot_general(a, b, dims, preferred_element_type=jnp.float32)
     filt_step = part(taps_hi, table_hi) + (part(taps_hi, table_lo) + part(taps_lo, table_hi))
-    sent_mix = from_partner(to_rows(grad_mix_cols), "pipe", 0).astype(jnp.float32)
+    token_rows = sent_parts[0].shape[0]
+    ctx_count = lax.axis_size("ctx")
+    sent_mix = jnp.stack(
+        [p.reshape(token_rows, ctx_count, width) for p in sent_parts], axis=2
+    ).reshape(token_rows, -1).astype(jnp.float32)
     rest = jnp.stack(
         [
             sent_mix * partner_kv[:, 1].astype(jnp.float32),

time: 302 us -> 300 us (level)
  waiting for transfers between devices: 88.9 us -> 79.1 us
  local copies, waits for them, and re-layouts: 35.8 us -> 39.6 us
    all_to_all x3 -> x4, waiting for transfers between devices: 41.4 us -> 31.3 us  [to_rows(): lax.all_to_all(columns, 'ctx', split_axis=0, concat_axis=1, tiled=True)]
    dot_general x9 -> x12, matrix products: 27.6 us -> 30.7 us  [dot_tt(): lax.dot_general(table, spec, (((1,), (0,)), ((), ())), preferred_element_...]
    all_to_all x3 -> x4, starting transfers between devices: 14.4 us -> 16.6 us  [to_rows(): lax.all_to_all(columns, 'ctx', split_axis=0, concat_axis=1, tiled=True)]
    unnamed x50 -> x60, local copies, waits for them, and re-layouts: 16.6 us -> 18.8 us
    ppermute x4 -> x5, waiting for transfers between devices: 12.3 us -> 12.5 us  [from_partner(): return lax.ppermute(block, axis, route)]
  transfers between devices with their start and end apart: 10 -> 12, of which waited for: 8 -> 9; matrix products, arithmetic and copies ran while one was open for 41% -> 43% of each run, Pallas kernels for 0% -> 0%
where the time goes in v3:
time: 300 us; the launch traced here: 295 us
  matrix products  84.8 us (28%)
  waiting for transfers between devices  79.1 us (26%)
  other arithmetic  47.3 us (16%)
  local copies, waits for them, and re-layouts  39.6 us (13%)
  starting transfers between devices  37.2 us (12%)
  blocking collectives  4.93 us (2%)
    all_to_all x3, waiting for transfers between devices, to_columns(): return lax.all_to_all(rows, 'ctx', split_axis=1, concat_axis=0, tiled=True)  35.3 us
    all_to_all x4, waiting for transfers between devices, to_rows(): lax.all_to_all(columns, 'ctx', split_axis=0, concat_axis=1, tiled=True)  31.3 us
    dot_general x12, matrix products, dot_tt(): lax.dot_general(table, spec, (((1,), (0,)), ((), ())), preferred_element_...  30.7 us
    dot_general x6, matrix products, dot_tf(): lax.dot_general(table, signal, (((0,), (0,)), ((), ())), preferred_elemen...  21.4 us
    unnamed x60, local copies, waits for them, and re-layouts  18.8 us
    dot_general x3, matrix products, on_device(): lax.dot_general(a, b, dims, preferred_element_type=jnp.float32)  18.3 us
    all_to_all x4, starting transfers between devices, to_rows(): lax.all_to_all(columns, 'ctx', split_axis=0, concat_axis=1, tiled=True)  16.6 us
    all_to_all x3, starting transfers between devices, to_columns(): return lax.all_to_all(rows, 'ctx', split_axis=1, concat_axis=0, tiled=True)  14.5 us
  transfers between devices with their start and end apart: 12, of which 9 were waited for; matrix products, arithmetic and copies ran while one was open for 43% of the time, Pallas kernels for 0%

profile of v3, /device:TPU:0, one launch (start us, length us, event | category | flops | bytes accessed | tf_op | source)
XLA Modules:
  0.0 294.5 jit_solution(6509432630752267123)
XLA Ops:
  0.6 3.5 %copy.23 = bf16[1,128,3,4096]{1,3,2,0:T(8,128)(2,1)S(1)} copy(bf16[1,128,3,4096]{3,1,2,0:T(8,128)(2,1)} %param.6) | data formatting | bytes 6291456 | tf_op args[1]
  5.6 2.9 collective-permute-start.1
  9.8 5.8 %all-to-all-start.2 = ((bf16[128,8,512]{0,2,1:T(8,128)(2,1)}), bf16[128,8,512]{0,2,1:T(8,128)(2,1)}, u32[]{:S(2)}, u32[]{:S(2)}) async-start(bf16[128,8,512]{0,2,1:T(8,128)(2,1)} %bitcast.134), calls=%async_computation.2 | async-start | bytes 2097152 | tf_op jit(solution)/shard_map/all_to_all | solution.py:265
  16.7 4.5 %multiply_subtract_fusion = (f32[32,32,1024]{2,1,0:T(8,128)}, f32[32,32,1024]{2,1,0:T(8,128)}) fusion(f32[32,1024]{1,0:T(8,128)S(1)} %get-tuple-element.42, f32[32,1024]{1,0:T(8,128)S(1)} %get-tuple-element.39, f32[32,1024]{1,0:T(8,128)S(1)} %get-tuple-element.43, f32[32,1024]{1,0:T(8,128)S(1)} %get-tuple-element.38), kind=kLoop, calls=%fused_computation.23 | loop fusion | flops 7340032 | bytes 8912896 | tf_op jit(solution)/shard_map/sub | solution.py:103
  21.2 4.6 %copy.20 = bf16[1,128,3,4096]{1,3,2,0:T(8,128)(2,1)} copy(bf16[1,128,3,4096]{3,1,2,0:T(8,128)(2,1)} %param.5) | data formatting | bytes 6291456 | tf_op args[0]
  25.9 2.8 bitcast_select_fusion
  29.3 4.2 %fusion = (bf16[1024,2048]{1,0:T(8,128)(2,1)}, bf16[1024,2048]{1,0:T(8,128)(2,1)}) fusion(f32[1024,1024]{1,0:T(8,128)S(1)} %bitcast_select_fusion, f32[1024,1024]{1,0:T(8,128)S(1)} %bitcast.131), kind=kLoop, calls=%fused_computation.2 | loop fusion | flops 10485760 | bytes 16777216 | tf_op jit(solution)/shard_map/convert_element_type | solution.py:85
  34.7 6.6 %all-to-all-done.2 = bf16[128,8,512]{0,2,1:T(8,128)(2,1)} async-done(((bf16[128,8,512]{0,2,1:T(8,128)(2,1)}), bf16[128,8,512]{0,2,1:T(8,128)(2,1)}, u32[]{:S(2)}, u32[]{:S(2)}) %all-to-all-start.2) | async-done | bytes 1048608 | tf_op jit(solution)/shard_map/all_to_all | solution.py:265
  41.3 4.4 %all-to-all-start = ((bf16[128,8,512]{0,2,1:T(8,128)(2,1)}), bf16[128,8,512]{0,2,1:T(8,128)(2,1)}, u32[]{:S(2)}, u32[]{:S(2)}) async-start(bf16[128,8,512]{0,2,1:T(8,128)(2,1)} %bitcast.135), calls=%async_computation | async-start | bytes 2097152 | tf_op jit(solution)/shard_map/all_to_all | solution.py:265
  45.8 5.5 %fusion.27 = f32[2048,512]{1,0:T(8,128)S(1)} fusion(bf16[1024,2048]{1,0:T(8,128)(2,1)} %get-tuple-element.27, f32[1,1,512,1024]{3,2,1,0:T(8,128)} %param.8), kind=kOutput, calls=%fused_computation.83 | convolution fusion | flops 2148532224 | bytes 10485760 | tf_op jit(solution)/shard_map/dot_general | solution.py:144
  51.3 2.4 fusion.26
  53.7 6.6 %broadcast_multiply_fusion = (f32[2048,512]{1,0:T(8,128)}, f32[2048,512]{1,0:T(8,128)}) fusion(f32[2048]{0:T(1024)S(1)} %select_multiply_fusion, f32[2048,512]{1,0:T(8,128)S(1)} %fusion.27, f32[2048,512]{1,0:T(8,128)S(1)} %fusion.26, bf16[1024,2048]{1,0:T(8,128)(2,1)S(1)} %copy-done, f32[1,1,512,1024]{3,2,1,0:T(8,128)S(1)} %copy-done.23), kind=kOutput, calls=%fused_computation.67 | convolution fusion | flops 2152202240 | bytes 23076864 | tf_op jit(solution)/shard_map/dot_general | solution.py:144
  60.3 2.3 copy.24
  62.6 8.6 %all-to-all-done = bf16[128,8,512]{0,2,1:T(8,128)(2,1)} async-done(((bf16[128,8,512]{0,2,1:T(8,128)(2,1)}), bf16[128,8,512]{0,2,1:T(8,128)(2,1)}, u32[]{:S(2)}, u32[]{:S(2)}) %all-to-all-start) | async-done | bytes 1048608 | tf_op jit(solution)/shard_map/all_to_all | solution.py:265
  71.2 2.5 copy.21
  73.7 5.1 %fusion.69 = f32[2048,512]{1,0:T(8,128)S(1)} fusion(bf16[1024,2048]{1,0:T(8,128)(2,1)} %get-tuple-element.27, bf16[1024,512]{1,0:T(8,128)(2,1)} %bitcast.140), kind=kOutput, calls=%fused_computation.137 | convolution fusion | flops 2147483648 | bytes 9437184 | tf_op jit(solution)/shard_map/dot_general | solution.py:118
  78.8 2.4 convolution_add_fusion.1
  81.2 2.4 fusion.70
  83.7 2.5 convolution_add_fusion
  86.3 3.7 %subtract_select_fusion = (f32[1024,512]{1,0:T(8,128)S(1)}, f32[1024,512]{1,0:T(8,128)S(1)}, f32[1024,512]{1,0:T(8,128)}, f32[1024,512]{1,0:T(8,128)}) fusion(f32[2048,512]{1,0:T(8,128)S(1)} %convolution_add_fusion, f32[2048,512]{1,0:T(8,128)S(1)} %copy-done.6, pred[1024]{0:T(1024)(128)(4,1)S(1)} %get-tuple-element.46, f32[2048,512]{1,0:T(8,128)S(1)} %convolution_add_fusion.1), kind=kLoop, calls=%fused_computation.27 | loop fusion | flops 8388608 | bytes 20972544 | tf_op jit(solution)/shard_map/jit(_where)/select_n | solution.py:165
  90.0 2.3 fusion.48
  92.3 2.3 fusion.47
  94.7 3.3 %add_convert_fusion = bf16[1024,512]{1,0:T(8,128)(2,1)} fusion(f32[1024,512]{1,0:T(8,128)S(1)} %fusion.48, f32[1024,512]{1,0:T(8,128)S(1)} %fusion.47, bf16[1024,2048]{1,0:T(8,128)(2,1)S(1)} %copy-done.1, f32[1024,512]{1,0:T(8,128)S(1)} %get-tuple-element.23, f32[1024,512]{1,0:T(8,128)S(1)} %get-tuple-element.22), kind=kOutput, calls=%fused_computation.60 | convolution fusion | flops 2153250816 | bytes 13631488 | tf_op jit(solution)/shard_map/dot_general | solution.py:124
  98.0 4.2 %all-to-all-start.3 = ((bf16[8,128,512]{2,1,0:T(8,128)(2,1)}), bf16[8,128,512]{2,1,0:T(8,128)(2,1)}, u32[]{:S(2)}, u32[]{:S(2)}) async-start(bf16[8,128,512]{2,1,0:T(8,128)(2,1)} %bitcast.139), calls=%async_computation.3 | async-start | bytes 2097152 | tf_op jit(solution)/shard_map/all_to_all | solution.py:268
  102.3 5.9 %fusion.46 = f32[1024,512]{1,0:T(8,128)S(1)} fusion(bf16[1024,2048]{1,0:T(8,128)(2,1)} %get-tuple-element.27, f32[1024,512]{1,0:T(8,128)} %get-tuple-element.30, f32[1024,512]{1,0:T(8,128)} %get-tuple-element.31), kind=kOutput, calls=%fused_computation.108 | convolution fusion | flops 2150629376 | bytes 10485760 | tf_op jit(solution)/shard_map/dot_general | solution.py:124
  108.2 2.3 fusion.45
  110.6 3.4 %add_convert_fusion.1 = bf16[1024,512]{1,0:T(8,128)(2,1)} fusion(f32[1024,512]{1,0:T(8,128)S(1)} %fusion.46, f32[1024,512]{1,0:T(8,128)S(1)} %fusion.45, bf16[1024,2048]{1,0:T(8,128)(2,1)S(1)} %copy-done.2, f32[1024,512]{1,0:T(8,128)S(1)} %copy-done.21, f32[1024,512]{1,0:T(8,128)S(1)} %copy-done.22), kind=kOutput, calls=%fused_computation.65 | convolution fusion | flops 2153250816 | bytes 13631488 | tf_op jit(solution)/shard_map/dot_general | solution.py:124
  113.9 13.7 %all-to-all-done.3 = bf16[8,128,512]{2,1,0:T(8,128)(2,1)} async-done(((bf16[8,128,512]{2,1,0:T(8,128)(2,1)}), bf16[8,128,512]{2,1,0:T(8,128)(2,1)}, u32[]{:S(2)}, u32[]{:S(2)}) %all-to-all-start.3) | async-done | bytes 1048608 | tf_op jit(solution)/shard_map/all_to_all | solution.py:268
  127.6 4.4 %all-to-all-start.1 = ((bf16[8,128,512]{2,1,0:T(8,128)(2,1)}), bf16[8,128,512]{2,1,0:T(8,128)(2,1)}, u32[]{:S(2)}, u32[]{:S(2)}) async-start(bf16[8,128,512]{2,1,0:T(8,128)(2,1)} %bitcast.136), calls=%async_computation.1 | async-start | bytes 2097152 | tf_op jit(solution)/shard_map/all_to_all | solution.py:268
  132.1 2.3 copy.26
  135.8 3.0 %copy.28 = f32[128,8,512]{2,0,1:T(8,128)} copy(f32[128,8,512]{0,2,1:T(8,128)} %bitcast.133) | data formatting | bytes 4194304 | tf_op jit(solution)/shard_map/convert_element_type | solution.py:289
  138.8 2.6 copy.27
  142.6 2.8 convert_bitcast_fusion
  145.4 2.9 copy.25
  148.4 9.1 %all-to-all-done.1 = bf16[8,128,512]{2,1,0:T(8,128)(2,1)} async-done(((bf16[8,128,512]{2,1,0:T(8,128)(2,1)}), bf16[8,128,512]{2,1,0:T(8,128)(2,1)}, u32[]{:S(2)}, u32[]{:S(2)}) %all-to-all-start.1) | async-done | bytes 1048608 | tf_op jit(solution)/shard_map/all_to_all | solution.py:268
  157.4 2.8 convert_bitcast_fusion.1
  160.3 2.9 copy.22
  163.2 2.6 multiply_reduce_fusion.2
  166.3 2.5 psum.22
  168.8 2.2 multiply_reduce_fusion
  171.0 2.5 all-reduce
  173.5 4.3 %multiply_convert_fusion.2 = bf16[128,8,512]{2,0,1:T(8,128)(2,1)} fusion(f32[128,8,512]{2,0,1:T(8,128)} %copy.28, f32[128,8,512]{2,0,1:T(8,128)} %copy.27, f32[128]{0:T(128)S(1)} %broadcast_multiply_fusion.1, f32[8,512]{1,0:T(8,128)S(1)} %mul.342, f32[128]{0:T(128)S(1)} %add_rsqrt_fusion, bf16[8,128,512]{2,1,0:T(8,128)(2,1)} %all-to-all-done.3), kind=kLoop, calls=%fused_computation.57 | loop fusion | flops 4718592 | bytes 6308864 | tf_op jit(solution)/shard_map/convert_element_type | solution.py:297
  177.8 4.3 %all-to-all-start.4 = ((bf16[128,8,512]{2,0,1:T(8,128)(2,1)}), bf16[128,8,512]{2,0,1:T(8,128)(2,1)}, u32[]{:S(2)}, u32[]{:S(2)}) async-start(bf16[128,8,512]{2,0,1:T(8,128)(2,1)} %multiply_convert_fusion.2), calls=%async_computation.4 | async-start | bytes 2097152 | tf_op jit(solution)/shard_map/all_to_all | solution.py:265
  182.1 4.3 %fusion.14 = (bf16[128,4096]{0,1:T(8,128)(2,1)}, bf16[128,4096]{0,1:T(8,128)(2,1)}) fusion(f32[128,8,512]{0,2,1:T(8,128)} %copy.25, bf16[1,128,4096]{1,2,0:T(8,128)(2,1)} %copy.26, f32[128]{0:T(128)S(1)} %broadcast_multiply_fusion.1, f32[128]{0:T(128)S(1)} %add_rsqrt_fusion, f32[4096]{0:T(1024)S(1)} %bitcast.148, bf16[128,3,4096]{0,2,1:T(8,128)(2,1)S(1)} %bitcast.126, ...), kind=kLoop, calls=%fused_computation.49 | loop fusion | flops 7864320 | bytes 9455104 | tf_op jit(solution)/shard_map/convert_element_type | solution.py:298
  188.4 20.1 %all-to-all-done.4 = bf16[128,8,512]{2,0,1:T(8,128)(2,1)} async-done(((bf16[128,8,512]{2,0,1:T(8,128)(2,1)}), bf16[128,8,512]{2,0,1:T(8,128)(2,1)}, u32[]{:S(2)}, u32[]{:S(2)}) %all-to-all-start.4) | async-done | bytes 1048608 | tf_op jit(solution)/shard_map/all_to_all | solution.py:265
  208.4 5.0 %fusion.71 = f32[2048,512]{1,0:T(8,128)S(1)} fusion(bf16[1024,2048]{1,0:T(8,128)(2,1)} %get-tuple-element.27, bf16[1024,512]{1,0:T(8,128)(2,1)} %bitcast.24), kind=kOutput, calls=%fused_computation.139 | convolution fusion | flops 2147483648 | bytes 9437184 | tf_op jit(solution)/shard_map/dot_general | solution.py:118
  213.5 3.9 %add_multiply_fusion = f32[2048,512]{1,0:T(8,128)S(1)} fusion(f32[2048,512]{1,0:T(8,128)S(1)} %fusion.71, bf16[1024,2048]{1,0:T(8,128)(2,1)S(1)} %copy-done.17, bf16[1024,512]{1,0:T(8,128)(2,1)} %bitcast.24, f32[2048]{0:T(1024)S(1)} %select_multiply_fusion), kind=kOutput, calls=%fused_computation.19 | convolution fusion | flops 2149580800 | bytes 13639680 | tf_op jit(solution)/shard_map/dot_general | solution.py:118
  217.5 2.9 add_select_fusion
  224.6 2.1 fusion.22
  228.0 2.0 copy.31
  230.0 4.4 %all-to-all-start.6 = ((bf16[8,128,256]{1,2,0:T(8,128)(2,1)}), bf16[8,128,256]{1,2,0:T(8,128)(2,1)}, u32[]{:S(2)}, u32[]{:S(2)}) async-start(bf16[8,128,256]{1,2,0:T(8,128)(2,1)} %copy.31), calls=%async_computation.6 | async-start | bytes 1048576 | tf_op jit(solution)/shard_map/all_to_all | solution.py:268
  234.4 3.9 %convolution_add_fusion.4 = f32[1024,256]{1,0:T(8,128)S(1)} fusion(f32[1024,256]{1,0:T(8,128)S(1)} %fusion.28, bf16[1024,2048]{1,0:T(8,128)(2,1)} %get-tuple-element.27, f32[1024,512]{1,0:T(8,128)S(1)} %get-tuple-element.28, f32[1024,512]{1,0:T(8,128)} %copy-done.8), kind=kOutput, calls=%fused_computation.75 | convolution fusion | flops 1076101120 | bytes 10485760 | tf_op jit(solution)/shard_map/dot_general | solution.py:124
  240.2 2.4 copy.33
  243.6 5.1 %all-to-all-done.6 = bf16[8,128,256]{1,2,0:T(8,128)(2,1)} async-done(((bf16[8,128,256]{1,2,0:T(8,128)(2,1)}), bf16[8,128,256]{1,2,0:T(8,128)(2,1)}, u32[]{:S(2)}, u32[]{:S(2)}) %all-to-all-start.6) | async-done | bytes 524320 | tf_op jit(solution)/shard_map/all_to_all | solution.py:268
  248.7 3.6 %all-to-all-start.5 = ((bf16[8,128,256]{1,2,0:T(8,128)(2,1)}), bf16[8,128,256]{1,2,0:T(8,128)(2,1)S(1)}, u32[]{:S(2)}, u32[]{:S(2)}) async-start(bf16[8,128,256]{1,2,0:T(8,128)(2,1)} %copy.30), calls=%async_computation.5 | async-start | bytes 1048576 | tf_op jit(solution)/shard_map/all_to_all | solution.py:268
  252.3 6.7 %fusion.50 = f32[512,1024]{1,0:T(8,128)} fusion(bf16[1024,2048]{1,0:T(8,128)(2,1)} %get-tuple-element.27, f32[1024,512]{1,0:T(8,128)} %get-tuple-element.19, f32[1024,512]{1,0:T(8,128)S(1)} %copy-done.19), kind=kOutput, calls=%fused_computation.112 | convolution fusion | flops 2150629376 | bytes 10485760 | tf_op jit(solution)/shard_map/dot_general | solution.py:314
  259.0 3.8 %fusion.49 = f32[512,1024]{1,0:T(8,128)} fusion(bf16[1024,2048]{1,0:T(8,128)(2,1)S(1)} %copy-done.18, f32[1024,512]{1,0:T(8,128)S(1)} %copy-done.20, f32[1024,512]{1,0:T(8,128)S(1)} %copy-done.19), kind=kOutput, calls=%fused_computation.111 | convolution fusion | flops 2150629376 | bytes 10485760 | tf_op jit(solution)/shard_map/dot_general | solution.py:314
  263.4 3.5 %all-to-all-done.5 = bf16[8,128,256]{1,2,0:T(8,128)(2,1)S(1)} async-done(((bf16[8,128,256]{1,2,0:T(8,128)(2,1)}), bf16[8,128,256]{1,2,0:T(8,128)(2,1)S(1)}, u32[]{:S(2)}, u32[]{:S(2)}) %all-to-all-start.5) | async-done | bytes 524320 | tf_op jit(solution)/shard_map/all_to_all | solution.py:268
  267.4 7.8 %add_bitcast_fusion = f32[1,1,512,1024]{3,2,1,0:T(8,128)} fusion(f32[512,1024]{1,0:T(8,128)} %fusion.50, f32[512,1024]{1,0:T(8,128)} %fusion.49, bf16[1024,2048]{1,0:T(8,128)(2,1)} %get-tuple-element.27, f32[1024,512]{1,0:T(8,128)} %get-tuple-element.19, f32[1024,512]{1,0:T(8,128)S(1)} %copy-done.19), kind=kOutput, calls=%fused_computation.52 | convolution fusion | flops 2152726528 | bytes 14680064 | tf_op jit(solution)/shard_map/dot_general | solution.py:314
  275.2 2.7 collective-permute-done.4
  277.9 9.8 %collective-permute-done.3 = bf16[128,2048]{0,1:T(8,128)(2,1)S(1)} collective-permute-done((bf16[128,2048]{0,1:T(8,128)(2,1)S(1)}, bf16[128,2048]{0,1:T(8,128)(2,1)S(1)}, u32[]{:S(2)}, u32[]{:S(2)}) %collective-permute-start.3) | collective-permute-done | bytes 524320 | tf_op jit(solution)/shard_map/ppermute | solution.py:19
  288.0 1.9 multiply_convert_fusion.1
  289.9 1.6 maximum_bitcast_fusion
  291.5 2.8 copy.34
  (86 shorter events, 20.7 us)
Async XLA Ops:
  5.6 75.6 %collective-permute-start.1 = (bf16[128,2,4096]{0,2,1:T(8,128)(2,1)}, bf16[128,2,4096]{0,2,1:T(8,128)(2,1)}, u32[]{:S(2)}, u32[]{:S(2)}) collective-permute-start(bf16[128,2,4096]{0,2,1:T(8,128)(2,1)} %slice.98), channel_id=1, source_target_pairs={{0,16},{16,0},{1,17},{17,1},{2,18},{18,2},{3,19},{19,3},{4,20},{20... | collective-permute-start | bytes 6291464 | tf_op jit(solution)/shard_map/ppermute | solution.py:19
  9.8 31.6 %all-to-all-start.2 = ((bf16[128,8,512]{0,2,1:T(8,128)(2,1)}), bf16[128,8,512]{0,2,1:T(8,128)(2,1)}, u32[]{:S(2)}, u32[]{:S(2)}) async-start(bf16[128,8,512]{0,2,1:T(8,128)(2,1)} %bitcast.134), calls=%async_computation.2 | async-start | bytes 2097152 | tf_op jit(solution)/shard_map/all_to_all | solution.py:265
  25.9 3.4 %copy-start.11 = (f32[32,32,1024]{2,1,0:T(8,128)S(1)}, f32[32,32,1024]{2,1,0:T(8,128)}, u32[]{:S(2)}) copy-start(f32[32,32,1024]{2,1,0:T(8,128)} %get-tuple-element.34) | copy-start | bytes 12582916
  29.3 4.2 %copy-start.10 = (bf16[1,128,3,4096]{1,3,2,0:T(8,128)(2,1)S(1)}, bf16[1,128,3,4096]{1,3,2,0:T(8,128)(2,1)}, u32[]{:S(2)}) copy-start(bf16[1,128,3,4096]{1,3,2,0:T(8,128)(2,1)} %copy.20) | copy-start | bytes 9437188
  41.3 29.9 %all-to-all-start = ((bf16[128,8,512]{0,2,1:T(8,128)(2,1)}), bf16[128,8,512]{0,2,1:T(8,128)(2,1)}, u32[]{:S(2)}, u32[]{:S(2)}) async-start(bf16[128,8,512]{0,2,1:T(8,128)(2,1)} %bitcast.135), calls=%async_computation | async-start | bytes 2097152 | tf_op jit(solution)/shard_map/all_to_all | solution.py:265
  45.8 5.5 %copy-start.14 = (bf16[1024,2048]{1,0:T(8,128)(2,1)S(1)}, bf16[1024,2048]{1,0:T(8,128)(2,1)}, u32[]{:S(2)}) copy-start(bf16[1024,2048]{1,0:T(8,128)(2,1)} %get-tuple-element.26) | copy-start | bytes 12582916
  45.8 5.5 %copy-start.23 = (f32[1,1,512,1024]{3,2,1,0:T(8,128)S(1)}, f32[1,1,512,1024]{3,2,1,0:T(8,128)}, u32[]{:S(2)}) copy-start(f32[1,1,512,1024]{3,2,1,0:T(8,128)} %param.8) | copy-start | bytes 6291460
  51.3 2.4 copy-start
  73.7 5.1 %copy-start.15 = (bf16[1024,2048]{1,0:T(8,128)(2,1)S(1)}, bf16[1024,2048]{1,0:T(8,128)(2,1)}, u32[]{:S(2)}) copy-start(bf16[1024,2048]{1,0:T(8,128)(2,1)} %get-tuple-element.26) | copy-start | bytes 12582916
  73.7 5.1 %copy-start.25 = (bf16[8,128,512]{2,1,0:T(8,128)(2,1)S(1)}, bf16[8,128,512]{2,1,0:T(8,128)(2,1)}, u32[]{:S(2)}) copy-start(bf16[8,128,512]{2,1,0:T(8,128)(2,1)} %copy.21) | copy-start | bytes 3145732
  78.8 2.4 copy-start.24
  81.2 2.5 copy-start.1
  83.7 2.6 copy-start.6
  86.2 3.7 %copy-start.12 = (f32[2048,512]{1,0:T(8,128)}, f32[2048,512]{1,0:T(8,128)S(1)}, u32[]{:S(2)}) copy-start(f32[2048,512]{1,0:T(8,128)S(1)} %convolution_add_fusion) | copy-start | bytes 12582916
  98.0 29.7 %all-to-all-start.3 = ((bf16[8,128,512]{2,1,0:T(8,128)(2,1)}), bf16[8,128,512]{2,1,0:T(8,128)(2,1)}, u32[]{:S(2)}, u32[]{:S(2)}) async-start(bf16[8,128,512]{2,1,0:T(8,128)(2,1)} %bitcast.139), calls=%async_computation.3 | async-start | bytes 2097152 | tf_op jit(solution)/shard_map/all_to_all | solution.py:268
  102.2 6.0 %copy-start.16 = (bf16[1024,2048]{1,0:T(8,128)(2,1)S(1)}, bf16[1024,2048]{1,0:T(8,128)(2,1)}, u32[]{:S(2)}) copy-start(bf16[1024,2048]{1,0:T(8,128)(2,1)} %get-tuple-element.26) | copy-start | bytes 12582916
  102.2 6.0 %copy-start.21 = (f32[1024,512]{1,0:T(8,128)S(1)}, f32[1024,512]{1,0:T(8,128)}, u32[]{:S(2)}) copy-start(f32[1024,512]{1,0:T(8,128)} %get-tuple-element.30) | copy-start | bytes 6291460
  102.3 6.0 %copy-start.22 = (f32[1024,512]{1,0:T(8,128)S(1)}, f32[1024,512]{1,0:T(8,128)}, u32[]{:S(2)}) copy-start(f32[1024,512]{1,0:T(8,128)} %get-tuple-element.31) | copy-start | bytes 6291460
  108.2 2.4 copy-start.2
  127.6 29.8 %all-to-all-start.1 = ((bf16[8,128,512]{2,1,0:T(8,128)(2,1)}), bf16[8,128,512]{2,1,0:T(8,128)(2,1)}, u32[]{:S(2)}, u32[]{:S(2)}) async-start(bf16[8,128,512]{2,1,0:T(8,128)(2,1)} %bitcast.136), calls=%async_computation.1 | async-start | bytes 2097152 | tf_op jit(solution)/shard_map/all_to_all | solution.py:268
  138.8 3.1 %copy-start.26 = (f32[1,4096]{1,0:T(1,128)S(1)}, f32[1,4096]{1,0:T(1,128)}, u32[]{:S(2)}) copy-start(f32[1,4096]{1,0:T(1,128)} %param.9) | copy-start | bytes 49156
  163.2 2.6 copy-start.7
  177.8 30.6 %all-to-all-start.4 = ((bf16[128,8,512]{2,0,1:T(8,128)(2,1)}), bf16[128,8,512]{2,0,1:T(8,128)(2,1)}, u32[]{:S(2)}, u32[]{:S(2)}) async-start(bf16[128,8,512]{2,0,1:T(8,128)(2,1)} %multiply_convert_fusion.2), calls=%async_computation.4 | async-start | bytes 2097152 | tf_op jit(solution)/shard_map/all_to_all | solution.py:265
  186.3 53.8 %collective-permute-start = (bf16[128,4096]{0,1:T(8,128)(2,1)}, bf16[128,4096]{0,1:T(8,128)(2,1)}, u32[]{:S(2)}, u32[]{:S(2)}) collective-permute-start(bf16[128,4096]{0,1:T(8,128)(2,1)} %get-tuple-element.37), channel_id=1, source_target_pairs={{0,16},{16,0},{1,17},{17,1},{2,18},{18,2},{3,19},{19,3},{4,20},{20... | collective-permute-start | bytes 3145736 | tf_op jit(solution)/shard_map/ppermute | solution.py:19
  186.9 53.3 %collective-permute-start.2 = (bf16[128,4096]{0,1:T(8,128)(2,1)}, bf16[128,4096]{0,1:T(8,128)(2,1)}, u32[]{:S(2)}, u32[]{:S(2)}) collective-permute-start(bf16[128,4096]{0,1:T(8,128)(2,1)} %get-tuple-element.36), channel_id=1, source_target_pairs={{0,16},{16,0},{1,17},{17,1},{2,18},{18,2},{3,19},{19,3},{4,20},{20... | collective-permute-start | bytes 3145736 | tf_op jit(solution)/shard_map/ppermute | solution.py:19
  208.4 5.0 %copy-start.17 = (bf16[1024,2048]{1,0:T(8,128)(2,1)S(1)}, bf16[1024,2048]{1,0:T(8,128)(2,1)}, u32[]{:S(2)}) copy-start(bf16[1024,2048]{1,0:T(8,128)(2,1)} %get-tuple-element.26) | copy-start | bytes 12582916
  213.5 4.0 %copy-start.5 = (f32[2048,512]{1,0:T(8,128)S(1)}, f32[2048,512]{1,0:T(8,128)}, u32[]{:S(2)}) copy-start(f32[2048,512]{1,0:T(8,128)} %get-tuple-element.41) | copy-start | bytes 12582916
  213.5 4.0 %copy-start.13 = (f32[2048,512]{1,0:T(8,128)S(1)}, f32[2048,512]{1,0:T(8,128)}, u32[]{:S(2)}) copy-start(f32[2048,512]{1,0:T(8,128)} %copy-done.12) | copy-start | bytes 12582916
  220.4 6.3 %copy-start.8 = (f32[1024,512]{1,0:T(8,128)}, f32[1024,512]{1,0:T(8,128)S(1)}, u32[]{:S(2)}) copy-start(f32[1024,512]{1,0:T(8,128)S(1)} %get-tuple-element.29) | copy-start | bytes 6291460
  220.5 2.8 copy-start.3
  230.0 18.7 %all-to-all-start.6 = ((bf16[8,128,256]{1,2,0:T(8,128)(2,1)}), bf16[8,128,256]{1,2,0:T(8,128)(2,1)}, u32[]{:S(2)}, u32[]{:S(2)}) async-start(bf16[8,128,256]{1,2,0:T(8,128)(2,1)} %copy.31), calls=%async_computation.6 | async-start | bytes 1048576 | tf_op jit(solution)/shard_map/all_to_all | solution.py:268
  234.4 3.9 %copy-start.4 = (bf16[1024,2048]{1,0:T(8,128)(2,1)S(1)}, bf16[1024,2048]{1,0:T(8,128)(2,1)}, u32[]{:S(2)}) copy-start(bf16[1024,2048]{1,0:T(8,128)(2,1)} %get-tuple-element.27) | copy-start | bytes 12582916
  234.4 4.4 %copy-start.9 = (f32[1024,512]{1,0:T(8,128)S(1)}, f32[1024,512]{1,0:T(8,128)}, u32[]{:S(2)}) copy-start(f32[1024,512]{1,0:T(8,128)} %copy-done.8) | copy-start | bytes 6291460
  240.2 12.2 %copy-start.19 = (f32[1024,512]{1,0:T(8,128)S(1)}, f32[1024,512]{1,0:T(8,128)}, u32[]{:S(2)}) copy-start(f32[1024,512]{1,0:T(8,128)} %get-tuple-element.18) | copy-start | bytes 6291460
  248.7 18.1 %all-to-all-start.5 = ((bf16[8,128,256]{1,2,0:T(8,128)(2,1)}), bf16[8,128,256]{1,2,0:T(8,128)(2,1)S(1)}, u32[]{:S(2)}, u32[]{:S(2)}) async-start(bf16[8,128,256]{1,2,0:T(8,128)(2,1)} %copy.30), calls=%async_computation.5 | async-start | bytes 1048576 | tf_op jit(solution)/shard_map/all_to_all | solution.py:268
  252.3 6.7 %copy-start.18 = (bf16[1024,2048]{1,0:T(8,128)(2,1)S(1)}, bf16[1024,2048]{1,0:T(8,128)(2,1)}, u32[]{:S(2)}) copy-start(bf16[1024,2048]{1,0:T(8,128)(2,1)} %get-tuple-element.26) | copy-start | bytes 12582916
  252.3 6.7 %copy-start.20 = (f32[1024,512]{1,0:T(8,128)S(1)}, f32[1024,512]{1,0:T(8,128)}, u32[]{:S(2)}) copy-start(f32[1024,512]{1,0:T(8,128)} %get-tuple-element.19) | copy-start | bytes 6291460
  262.8 15.1 %collective-permute-start.4 = (bf16[128,2048]{0,1:T(8,128)(2,1)}, bf16[128,2048]{0,1:T(8,128)(2,1)S(1)}, u32[]{:S(2)}, u32[]{:S(2)}) collective-permute-start(bf16[128,2048]{0,1:T(8,128)(2,1)} %bitcast.34), channel_id=1, source_target_pairs={{0,16},{16,0},{1,17},{17,1},{2,18},{18,2},{3,19},{19,3},{4,20},{20... | collective-permute-start | bytes 1572872 | tf_op jit(solution)/shard_map/ppermute | solution.py:19
  266.8 20.9 %collective-permute-start.3 = (bf16[128,2048]{0,1:T(8,128)(2,1)S(1)}, bf16[128,2048]{0,1:T(8,128)(2,1)S(1)}, u32[]{:S(2)}, u32[]{:S(2)}) collective-permute-start(bf16[128,2048]{0,1:T(8,128)(2,1)S(1)} %bitcast.142), channel_id=1, source_target_pairs={{0,16},{16,0},{1,17},{17,1},{2,18},{18,2},{3,19},{19,3},{4,20},{20... | collective-permute-start | bytes 1572872 | tf_op jit(solution)/shard_map/ppermute | solution.py:19

commit v4 on v3

--- a/solution.py
+++ b/solution.py
@@ -273,19 +273,11 @@
     partner_kv = from_partner(backward_rows[:, 1:3], "pipe", 0)
     forward_cols = to_columns(featurize(forward_rows))
     backward_cols = to_columns(featurize(backward_rows))
-    forward_spec = dense_spectrum_exact(forward_cols, table)
-    forward_z = to_rows(
-        dense_signal(dense_multiply(forward_spec, tap_scaled, False), table).astype(jnp.bfloat16)
-    )
     partner_kv, backward_cols = lax.optimization_barrier((partner_kv, backward_cols))
     backward_spec = dense_spectrum_exact(backward_cols, table)
     backward_z = to_rows(
         dense_signal(dense_multiply(backward_spec, tap_scaled, False), table).astype(jnp.bfloat16)
     )
-    forward_y = forward_rows[:, 0].astype(jnp.float32) * forward_z.astype(jnp.float32)
-    forward_scale = lax.rsqrt(row_total(forward_y * forward_y) / model_width + epsilon)[:, None]
-    forward_out = (forward_y * forward_scale * gain_row).astype(jnp.bfloat16)
-    sent_rows = from_partner(forward_out, "pipe", 0)
     backward_q = backward_rows[:, 0].astype(jnp.float32)
     conv_value = backward_z.astype(jnp.float32)
     backward_y = backward_q * conv_value
@@ -297,16 +289,27 @@
     grad_z = (grad_y * backward_q).astype(jnp.bfloat16)
     sent_first = from_partner((grad_y * conv_value).astype(jnp.bfloat16), "pipe", 0)
     grad_cols = to_columns(grad_z)
+    forward_cols, grad_z = lax.optimization_barrier((forward_cols, grad_z))
+    forward_spec = dense_spectrum_exact(forward_cols, table)
+    forward_z = to_rows(
+        dense_signal(dense_multiply(forward_spec, tap_scaled, False), table).astype(jnp.bfloat16)
+    )
+    forward_y = forward_rows[:, 0].astype(jnp.float32) * forward_z.astype(jnp.float32)
+    forward_scale = lax.rsqrt(row_total(forward_y * forward_y) / model_width + epsilon)[:, None]
+    forward_out = (forward_y * forward_scale * gain_row).astype(jnp.bfloat16)
+    sent_rows = from_partner(forward_out, "pipe", 0)
     grad_spec = dense_spectrum_exact(grad_cols, table) * weights
     mix_prod = dense_multiply(grad_spec, tap_spec, True)
     width = mix_prod.shape[1] // 2 if mix_prod.shape[1] % 256 == 0 else mix_prod.shape[1]
     pieces = mix_prod.shape[1] // width
     first_cols = dense_signal(mix_prod[:, :width], table).astype(jnp.bfloat16)
-    sent_rows, sent_first, first_cols = lax.optimization_barrier((sent_rows, sent_first, first_cols))
+    sent_first, first_cols = lax.optimization_barrier((sent_first, first_cols))
     sent_parts = [from_partner(to_rows(first_cols), "pipe", 0)]
     for piece in range(1, pieces):
         piece_cols = dense_signal(mix_prod[:, piece * width : (piece + 1) * width], table)
-        sent_parts.append(from_partner(to_rows(piece_cols.astype(jnp.bfloat16)), "pipe", 0))
+        piece_rows = to_rows(piece_cols.astype(jnp.bfloat16))
+        sent_rows, piece_rows = lax.optimization_barrier((sent_rows, piece_rows))
+        sent_parts.append(from_partner(piece_rows, "pipe", 0))
     taps_prod = dense_multiply(grad_spec, backward_spec, True)
     taps_hi, taps_lo = split_bf16(taps_prod)
     table_hi, table_lo = table

time: 300 us -> 300 us (level)
  no operation moved by 1% of the time
where the time goes in v4:
time: 300 us; the launch traced here: 295 us
  matrix products  85.3 us (28%)
  waiting for transfers between devices  76.5 us (26%)
  other arithmetic  48.3 us (16%)
  local copies, waits for them, and re-layouts  41.2 us (14%)
  starting transfers between devices  37.2 us (12%)
  blocking collectives  4.93 us (2%)
    all_to_all x3, waiting for transfers between devices, to_columns(): return lax.all_to_all(rows, 'ctx', split_axis=1, concat_axis=0, tiled=True)  35.3 us
    dot_general x12, matrix products, dot_tt(): lax.dot_general(table, spec, (((1,), (0,)), ((), ())), preferred_element_...  31.2 us
    all_to_all x4, waiting for transfers between devices, to_rows(): lax.all_to_all(columns, 'ctx', split_axis=0, concat_axis=1, tiled=True)  30.8 us
    dot_general x6, matrix products, dot_tf(): lax.dot_general(table, signal, (((0,), (0,)), ((), ())), preferred_elemen...  21.4 us
    unnamed x60, local copies, waits for them, and re-layouts  19.2 us
    dot_general x3, matrix products, on_device(): lax.dot_general(a, b, dims, preferred_element_type=jnp.float32)  18.3 us
    all_to_all x4, starting transfers between devices, to_rows(): lax.all_to_all(columns, 'ctx', split_axis=0, concat_axis=1, tiled=True)  16.6 us
    all_to_all x3, starting transfers between devices, to_columns(): return lax.all_to_all(rows, 'ctx', split_axis=1, concat_axis=0, tiled=True)  14.5 us
  transfers between devices with their start and end apart: 12, of which 9 were waited for; matrix products, arithmetic and copies ran while one was open for 43% of the time, Pallas kernels for 0%

profile of v4, /device:TPU:0, one launch (start us, length us, event | category | flops | bytes accessed | tf_op | source)
XLA Modules:
  0.0 294.9 jit_solution(17926792819637456601)
XLA Ops:
  0.6 3.5 %copy.23 = bf16[1,128,3,4096]{1,3,2,0:T(8,128)(2,1)S(1)} copy(bf16[1,128,3,4096]{3,1,2,0:T(8,128)(2,1)} %param.6) | data formatting | bytes 6291456 | tf_op args[1]
  5.6 2.9 collective-permute-start.1
  9.8 5.8 %all-to-all-start.2 = ((bf16[128,8,512]{0,2,1:T(8,128)(2,1)}), bf16[128,8,512]{0,2,1:T(8,128)(2,1)}, u32[]{:S(2)}, u32[]{:S(2)}) async-start(bf16[128,8,512]{0,2,1:T(8,128)(2,1)} %bitcast.134), calls=%async_computation.2 | async-start | bytes 2097152 | tf_op jit(solution)/shard_map/all_to_all | solution.py:265
  16.7 4.5 %multiply_subtract_fusion = (f32[32,32,1024]{2,1,0:T(8,128)}, f32[32,32,1024]{2,1,0:T(8,128)}) fusion(f32[32,1024]{1,0:T(8,128)S(1)} %get-tuple-element.44, f32[32,1024]{1,0:T(8,128)S(1)} %get-tuple-element.41, f32[32,1024]{1,0:T(8,128)S(1)} %get-tuple-element.45, f32[32,1024]{1,0:T(8,128)S(1)} %get-tuple-element.40), kind=kLoop, calls=%fused_computation.23 | loop fusion | flops 7340032 | bytes 8912896 | tf_op jit(solution)/shard_map/sub | solution.py:103
  21.2 4.6 %copy.20 = bf16[1,128,3,4096]{1,3,2,0:T(8,128)(2,1)} copy(bf16[1,128,3,4096]{3,1,2,0:T(8,128)(2,1)} %param.5) | data formatting | bytes 6291456 | tf_op args[0]
  25.9 2.8 bitcast_select_fusion
  29.3 4.2 %fusion = (bf16[1024,2048]{1,0:T(8,128)(2,1)}, bf16[1024,2048]{1,0:T(8,128)(2,1)}) fusion(f32[1024,1024]{1,0:T(8,128)S(1)} %bitcast_select_fusion, f32[1024,1024]{1,0:T(8,128)S(1)} %bitcast.131), kind=kLoop, calls=%fused_computation.2 | loop fusion | flops 10485760 | bytes 16777216 | tf_op jit(solution)/shard_map/convert_element_type | solution.py:85
  34.7 6.6 %all-to-all-done.2 = bf16[128,8,512]{0,2,1:T(8,128)(2,1)} async-done(((bf16[128,8,512]{0,2,1:T(8,128)(2,1)}), bf16[128,8,512]{0,2,1:T(8,128)(2,1)}, u32[]{:S(2)}, u32[]{:S(2)}) %all-to-all-start.2) | async-done | bytes 1048608 | tf_op jit(solution)/shard_map/all_to_all | solution.py:265
  41.3 4.4 %all-to-all-start = ((bf16[128,8,512]{0,2,1:T(8,128)(2,1)}), bf16[128,8,512]{0,2,1:T(8,128)(2,1)}, u32[]{:S(2)}, u32[]{:S(2)}) async-start(bf16[128,8,512]{0,2,1:T(8,128)(2,1)} %bitcast.135), calls=%async_computation | async-start | bytes 2097152 | tf_op jit(solution)/shard_map/all_to_all | solution.py:265
  45.8 5.5 %fusion.27 = f32[2048,512]{1,0:T(8,128)S(1)} fusion(bf16[1024,2048]{1,0:T(8,128)(2,1)} %get-tuple-element.29, f32[1,1,512,1024]{3,2,1,0:T(8,128)} %param.8), kind=kOutput, calls=%fused_computation.83 | convolution fusion | flops 2148532224 | bytes 10485760 | tf_op jit(solution)/shard_map/dot_general | solution.py:144
  51.3 2.4 fusion.26
  53.7 6.6 %broadcast_multiply_fusion = (f32[2048,512]{1,0:T(8,128)}, f32[2048,512]{1,0:T(8,128)}) fusion(f32[2048]{0:T(1024)S(1)} %select_multiply_fusion, f32[2048,512]{1,0:T(8,128)S(1)} %fusion.27, f32[2048,512]{1,0:T(8,128)S(1)} %fusion.26, bf16[1024,2048]{1,0:T(8,128)(2,1)S(1)} %copy-done, f32[1,1,512,1024]{3,2,1,0:T(8,128)S(1)} %copy-done.23), kind=kOutput, calls=%fused_computation.67 | convolution fusion | flops 2152202240 | bytes 23076864 | tf_op jit(solution)/shard_map/dot_general | solution.py:144
  60.3 2.3 copy.24
  62.6 8.6 %all-to-all-done = bf16[128,8,512]{0,2,1:T(8,128)(2,1)} async-done(((bf16[128,8,512]{0,2,1:T(8,128)(2,1)}), bf16[128,8,512]{0,2,1:T(8,128)(2,1)}, u32[]{:S(2)}, u32[]{:S(2)}) %all-to-all-start) | async-done | bytes 1048608 | tf_op jit(solution)/shard_map/all_to_all | solution.py:265
  71.2 2.5 copy.21
  73.7 5.1 %fusion.69 = f32[2048,512]{1,0:T(8,128)S(1)} fusion(bf16[1024,2048]{1,0:T(8,128)(2,1)} %get-tuple-element.29, bf16[1024,512]{1,0:T(8,128)(2,1)} %bitcast.140), kind=kOutput, calls=%fused_computation.137 | convolution fusion | flops 2147483648 | bytes 9437184 | tf_op jit(solution)/shard_map/dot_general | solution.py:118
  78.8 2.4 convolution_add_fusion.1
  81.2 2.4 fusion.70
  83.7 2.5 convolution_add_fusion
  86.3 3.7 %subtract_select_fusion = (f32[1024,512]{1,0:T(8,128)S(1)}, f32[1024,512]{1,0:T(8,128)S(1)}, f32[1024,512]{1,0:T(8,128)}, f32[1024,512]{1,0:T(8,128)}) fusion(f32[2048,512]{1,0:T(8,128)S(1)} %convolution_add_fusion, f32[2048,512]{1,0:T(8,128)S(1)} %copy-done.6, pred[1024]{0:T(1024)(128)(4,1)S(1)} %get-tuple-element.48, f32[2048,512]{1,0:T(8,128)S(1)} %convolution_add_fusion.1), kind=kLoop, calls=%fused_computation.27 | loop fusion | flops 8388608 | bytes 20972544 | tf_op jit(solution)/shard_map/jit(_where)/select_n | solution.py:165
  89.9 2.3 fusion.48
  92.3 2.3 fusion.47
  94.6 3.3 %add_convert_fusion = bf16[1024,512]{1,0:T(8,128)(2,1)} fusion(f32[1024,512]{1,0:T(8,128)S(1)} %fusion.48, f32[1024,512]{1,0:T(8,128)S(1)} %fusion.47, bf16[1024,2048]{1,0:T(8,128)(2,1)S(1)} %copy-done.1, f32[1024,512]{1,0:T(8,128)S(1)} %get-tuple-element.25, f32[1024,512]{1,0:T(8,128)S(1)} %get-tuple-element.24), kind=kOutput, calls=%fused_computation.60 | convolution fusion | flops 2153250816 | bytes 13631488 | tf_op jit(solution)/shard_map/dot_general | solution.py:124
  97.9 4.2 %all-to-all-start.3 = ((bf16[8,128,512]{2,1,0:T(8,128)(2,1)}), bf16[8,128,512]{2,1,0:T(8,128)(2,1)}, u32[]{:S(2)}, u32[]{:S(2)}) async-start(bf16[8,128,512]{2,1,0:T(8,128)(2,1)} %bitcast.139), calls=%async_computation.3 | async-start | bytes 2097152 | tf_op jit(solution)/shard_map/all_to_all | solution.py:268
  102.2 5.9 %fusion.46 = f32[1024,512]{1,0:T(8,128)S(1)} fusion(bf16[1024,2048]{1,0:T(8,128)(2,1)} %get-tuple-element.29, f32[1024,512]{1,0:T(8,128)} %get-tuple-element.32, f32[1024,512]{1,0:T(8,128)} %get-tuple-element.33), kind=kOutput, calls=%fused_computation.108 | convolution fusion | flops 2150629376 | bytes 10485760 | tf_op jit(solution)/shard_map/dot_general | solution.py:124
  108.2 2.3 fusion.45
  110.5 3.4 %add_convert_fusion.1 = bf16[1024,512]{1,0:T(8,128)(2,1)} fusion(f32[1024,512]{1,0:T(8,128)S(1)} %fusion.46, f32[1024,512]{1,0:T(8,128)S(1)} %fusion.45, bf16[1024,2048]{1,0:T(8,128)(2,1)S(1)} %copy-done.2, f32[1024,512]{1,0:T(8,128)S(1)} %copy-done.21, f32[1024,512]{1,0:T(8,128)S(1)} %copy-done.22), kind=kOutput, calls=%fused_computation.65 | convolution fusion | flops 2153250816 | bytes 13631488 | tf_op jit(solution)/shard_map/dot_general | solution.py:124
  113.9 13.7 %all-to-all-done.3 = bf16[8,128,512]{2,1,0:T(8,128)(2,1)} async-done(((bf16[8,128,512]{2,1,0:T(8,128)(2,1)}), bf16[8,128,512]{2,1,0:T(8,128)(2,1)}, u32[]{:S(2)}, u32[]{:S(2)}) %all-to-all-start.3) | async-done | bytes 1048608 | tf_op jit(solution)/shard_map/all_to_all | solution.py:268
  127.6 4.4 %all-to-all-start.1 = ((bf16[8,128,512]{2,1,0:T(8,128)(2,1)}), bf16[8,128,512]{2,1,0:T(8,128)(2,1)}, u32[]{:S(2)}, u32[]{:S(2)}) async-start(bf16[8,128,512]{2,1,0:T(8,128)(2,1)} %bitcast.136), calls=%async_computation.1 | async-start | bytes 2097152 | tf_op jit(solution)/shard_map/all_to_all | solution.py:268
  132.0 2.3 copy.26
  135.7 3.0 %copy.28 = f32[128,8,512]{2,0,1:T(8,128)} copy(f32[128,8,512]{0,2,1:T(8,128)} %bitcast.133) | data formatting | bytes 4194304 | tf_op jit(solution)/shard_map/convert_element_type | solution.py:281
  138.7 2.6 copy.27
  142.6 2.8 convert_bitcast_fusion
  145.4 2.9 copy.25
  148.3 9.1 %all-to-all-done.1 = bf16[8,128,512]{2,1,0:T(8,128)(2,1)} async-done(((bf16[8,128,512]{2,1,0:T(8,128)(2,1)}), bf16[8,128,512]{2,1,0:T(8,128)(2,1)}, u32[]{:S(2)}, u32[]{:S(2)}) %all-to-all-start.1) | async-done | bytes 1048608 | tf_op jit(solution)/shard_map/all_to_all | solution.py:268
  157.4 2.8 convert_bitcast_fusion.1
  160.2 2.9 copy.22
  163.1 2.6 multiply_reduce_fusion.2
  166.2 2.5 psum.22
  168.7 2.2 multiply_reduce_fusion
  170.9 2.5 all-reduce
  173.4 4.3 %multiply_convert_fusion.2 = bf16[128,8,512]{2,0,1:T(8,128)(2,1)} fusion(f32[128,8,512]{2,0,1:T(8,128)} %copy.28, f32[128,8,512]{2,0,1:T(8,128)} %copy.27, f32[128]{0:T(128)S(1)} %broadcast_multiply_fusion.1, f32[8,512]{1,0:T(8,128)S(1)} %mul.334, f32[128]{0:T(128)S(1)} %add_rsqrt_fusion, bf16[8,128,512]{2,1,0:T(8,128)(2,1)} %all-to-all-done.3), kind=kLoop, calls=%fused_computation.57 | loop fusion | flops 4718592 | bytes 6308864 | tf_op jit(solution)/shard_map/convert_element_type | solution.py:289
  177.7 4.3 %all-to-all-start.4 = ((bf16[128,8,512]{2,0,1:T(8,128)(2,1)}), bf16[128,8,512]{2,0,1:T(8,128)(2,1)}, u32[]{:S(2)}, u32[]{:S(2)}) async-start(bf16[128,8,512]{2,0,1:T(8,128)(2,1)} %multiply_convert_fusion.2), calls=%async_computation.4 | async-start | bytes 2097152 | tf_op jit(solution)/shard_map/all_to_all | solution.py:265
  182.0 4.3 %fusion.14 = (bf16[128,4096]{0,1:T(8,128)(2,1)}, bf16[128,4096]{0,1:T(8,128)(2,1)}) fusion(f32[128,8,512]{0,2,1:T(8,128)} %copy.25, bf16[1,128,4096]{1,2,0:T(8,128)(2,1)} %copy.26, f32[128]{0:T(128)S(1)} %broadcast_multiply_fusion.1, f32[128]{0:T(128)S(1)} %add_rsqrt_fusion, f32[4096]{0:T(1024)S(1)} %bitcast.147, bf16[128,3,4096]{0,2,1:T(8,128)(2,1)S(1)} %bitcast.126, ...), kind=kLoop, calls=%fused_computation.49 | loop fusion | flops 7864320 | bytes 9455104 | tf_op jit(solution)/shard_map/convert_element_type | solution.py:290
  188.3 20.1 %all-to-all-done.4 = bf16[128,8,512]{2,0,1:T(8,128)(2,1)} async-done(((bf16[128,8,512]{2,0,1:T(8,128)(2,1)}), bf16[128,8,512]{2,0,1:T(8,128)(2,1)}, u32[]{:S(2)}, u32[]{:S(2)}) %all-to-all-start.4) | async-done | bytes 1048608 | tf_op jit(solution)/shard_map/all_to_all | solution.py:265
  208.4 5.0 %fusion.71 = f32[2048,512]{1,0:T(8,128)S(1)} fusion(bf16[1024,2048]{1,0:T(8,128)(2,1)} %get-tuple-element.29, bf16[1024,512]{1,0:T(8,128)(2,1)} %bitcast.24), kind=kOutput, calls=%fused_computation.139 | convolution fusion | flops 2147483648 | bytes 9437184 | tf_op jit(solution)/shard_map/dot_general | solution.py:118
  213.4 3.9 %add_multiply_fusion = f32[2048,512]{1,0:T(8,128)S(1)} fusion(f32[2048,512]{1,0:T(8,128)S(1)} %fusion.71, bf16[1024,2048]{1,0:T(8,128)(2,1)S(1)} %copy-done.17, bf16[1024,512]{1,0:T(8,128)(2,1)} %bitcast.24, f32[2048]{0:T(1024)S(1)} %select_multiply_fusion), kind=kOutput, calls=%fused_computation.19 | convolution fusion | flops 2149580800 | bytes 13639680 | tf_op jit(solution)/shard_map/dot_general | solution.py:118
  217.4 2.9 add_select_fusion
  221.8 2.0 copy-done.3
  225.1 2.1 fusion.21
  227.2 2.0 copy.30
  229.3 4.4 %all-to-all-start.5 = ((bf16[8,128,256]{1,2,0:T(8,128)(2,1)}), bf16[8,128,256]{1,2,0:T(8,128)(2,1)}, u32[]{:S(2)}, u32[]{:S(2)}) async-start(bf16[8,128,256]{1,2,0:T(8,128)(2,1)} %copy.30), calls=%async_computation.5 | async-start | bytes 1048576 | tf_op jit(solution)/shard_map/all_to_all | solution.py:268
  233.7 3.6 %fusion.72 = f32[1024,256]{1,0:T(8,128)S(1)} fusion(bf16[1024,2048]{1,0:T(8,128)(2,1)} %get-tuple-element.28, bf16[2048,256]{1,0:T(8,128)(2,1)S(1)} %reduce-precision_convert_fusion.4), kind=kOutput, calls=%fused_computation.140 | convolution fusion | flops 1073741824 | bytes 6291456 | tf_op jit(solution)/shard_map/dot_general | solution.py:124
  239.0 2.1 fusion.22
  241.1 2.2 copy.31
  243.3 4.6 %all-to-all-done.5 = bf16[8,128,256]{1,2,0:T(8,128)(2,1)} async-done(((bf16[8,128,256]{1,2,0:T(8,128)(2,1)}), bf16[8,128,256]{1,2,0:T(8,128)(2,1)}, u32[]{:S(2)}, u32[]{:S(2)}) %all-to-all-start.5) | async-done | bytes 524320 | tf_op jit(solution)/shard_map/all_to_all | solution.py:268
  247.9 3.6 %all-to-all-start.6 = ((bf16[8,128,256]{1,2,0:T(8,128)(2,1)}), bf16[8,128,256]{1,2,0:T(8,128)(2,1)S(1)}, u32[]{:S(2)}, u32[]{:S(2)}) async-start(bf16[8,128,256]{1,2,0:T(8,128)(2,1)} %copy.31), calls=%async_computation.6 | async-start | bytes 1048576 | tf_op jit(solution)/shard_map/all_to_all | solution.py:268
  251.6 6.7 %fusion.50 = f32[512,1024]{1,0:T(8,128)} fusion(bf16[1024,2048]{1,0:T(8,128)(2,1)} %get-tuple-element.29, f32[1024,512]{1,0:T(8,128)} %get-tuple-element.21, f32[1024,512]{1,0:T(8,128)S(1)} %copy-done.19), kind=kOutput, calls=%fused_computation.112 | convolution fusion | flops 2150629376 | bytes 10485760 | tf_op jit(solution)/shard_map/dot_general | solution.py:317
  258.2 3.8 %fusion.49 = f32[512,1024]{1,0:T(8,128)} fusion(bf16[1024,2048]{1,0:T(8,128)(2,1)S(1)} %copy-done.18, f32[1024,512]{1,0:T(8,128)S(1)} %copy-done.20, f32[1024,512]{1,0:T(8,128)S(1)} %copy-done.19), kind=kOutput, calls=%fused_computation.111 | convolution fusion | flops 2150629376 | bytes 10485760 | tf_op jit(solution)/shard_map/dot_general | solution.py:317
  262.6 3.5 %all-to-all-done.6 = bf16[8,128,256]{1,2,0:T(8,128)(2,1)S(1)} async-done(((bf16[8,128,256]{1,2,0:T(8,128)(2,1)}), bf16[8,128,256]{1,2,0:T(8,128)(2,1)S(1)}, u32[]{:S(2)}, u32[]{:S(2)}) %all-to-all-start.6) | async-done | bytes 524320 | tf_op jit(solution)/shard_map/all_to_all | solution.py:268
  266.6 7.8 %add_bitcast_fusion = f32[1,1,512,1024]{3,2,1,0:T(8,128)} fusion(f32[512,1024]{1,0:T(8,128)} %fusion.50, f32[512,1024]{1,0:T(8,128)} %fusion.49, bf16[1024,2048]{1,0:T(8,128)(2,1)} %get-tuple-element.29, f32[1024,512]{1,0:T(8,128)} %get-tuple-element.21, f32[1024,512]{1,0:T(8,128)S(1)} %copy-done.19), kind=kOutput, calls=%fused_computation.52 | convolution fusion | flops 2152726528 | bytes 14680064 | tf_op jit(solution)/shard_map/dot_general | solution.py:317
  274.4 2.3 copy.33
  277.1 9.9 %collective-permute-done.3 = bf16[128,2048]{0,1:T(8,128)(2,1)} collective-permute-done((bf16[128,2048]{0,1:T(8,128)(2,1)S(1)}, bf16[128,2048]{0,1:T(8,128)(2,1)}, u32[]{:S(2)}, u32[]{:S(2)}) %collective-permute-start.3) | collective-permute-done | bytes 524320 | tf_op jit(solution)/shard_map/ppermute | solution.py:19
  291.9 2.8 copy.34
  (86 shorter events, 21.9 us)
Async XLA Ops:
  5.6 75.6 %collective-permute-start.1 = (bf16[128,2,4096]{0,2,1:T(8,128)(2,1)}, bf16[128,2,4096]{0,2,1:T(8,128)(2,1)}, u32[]{:S(2)}, u32[]{:S(2)}) collective-permute-start(bf16[128,2,4096]{0,2,1:T(8,128)(2,1)} %slice.98), channel_id=1, source_target_pairs={{0,16},{16,0},{1,17},{17,1},{2,18},{18,2},{3,19},{19,3},{4,20},{20... | collective-permute-start | bytes 6291464 | tf_op jit(solution)/shard_map/ppermute | solution.py:19
  9.8 31.6 %all-to-all-start.2 = ((bf16[128,8,512]{0,2,1:T(8,128)(2,1)}), bf16[128,8,512]{0,2,1:T(8,128)(2,1)}, u32[]{:S(2)}, u32[]{:S(2)}) async-start(bf16[128,8,512]{0,2,1:T(8,128)(2,1)} %bitcast.134), calls=%async_computation.2 | async-start | bytes 2097152 | tf_op jit(solution)/shard_map/all_to_all | solution.py:265
  25.9 3.4 %copy-start.11 = (f32[32,32,1024]{2,1,0:T(8,128)S(1)}, f32[32,32,1024]{2,1,0:T(8,128)}, u32[]{:S(2)}) copy-start(f32[32,32,1024]{2,1,0:T(8,128)} %get-tuple-element.36) | copy-start | bytes 12582916
  29.3 4.2 %copy-start.10 = (bf16[1,128,3,4096]{1,3,2,0:T(8,128)(2,1)S(1)}, bf16[1,128,3,4096]{1,3,2,0:T(8,128)(2,1)}, u32[]{:S(2)}) copy-start(bf16[1,128,3,4096]{1,3,2,0:T(8,128)(2,1)} %copy.20) | copy-start | bytes 9437188
  41.3 29.9 %all-to-all-start = ((bf16[128,8,512]{0,2,1:T(8,128)(2,1)}), bf16[128,8,512]{0,2,1:T(8,128)(2,1)}, u32[]{:S(2)}, u32[]{:S(2)}) async-start(bf16[128,8,512]{0,2,1:T(8,128)(2,1)} %bitcast.135), calls=%async_computation | async-start | bytes 2097152 | tf_op jit(solution)/shard_map/all_to_all | solution.py:265
  45.8 5.5 %copy-start.14 = (bf16[1024,2048]{1,0:T(8,128)(2,1)S(1)}, bf16[1024,2048]{1,0:T(8,128)(2,1)}, u32[]{:S(2)}) copy-start(bf16[1024,2048]{1,0:T(8,128)(2,1)} %get-tuple-element.28) | copy-start | bytes 12582916
  45.8 5.5 %copy-start.23 = (f32[1,1,512,1024]{3,2,1,0:T(8,128)S(1)}, f32[1,1,512,1024]{3,2,1,0:T(8,128)}, u32[]{:S(2)}) copy-start(f32[1,1,512,1024]{3,2,1,0:T(8,128)} %param.8) | copy-start | bytes 6291460
  51.3 2.4 copy-start
  73.7 5.1 %copy-start.15 = (bf16[1024,2048]{1,0:T(8,128)(2,1)S(1)}, bf16[1024,2048]{1,0:T(8,128)(2,1)}, u32[]{:S(2)}) copy-start(bf16[1024,2048]{1,0:T(8,128)(2,1)} %get-tuple-element.28) | copy-start | bytes 12582916
  73.7 5.1 %copy-start.25 = (bf16[8,128,512]{2,1,0:T(8,128)(2,1)S(1)}, bf16[8,128,512]{2,1,0:T(8,128)(2,1)}, u32[]{:S(2)}) copy-start(bf16[8,128,512]{2,1,0:T(8,128)(2,1)} %copy.21) | copy-start | bytes 3145732
  78.8 2.4 copy-start.24
  81.2 2.5 copy-start.1
  83.7 2.6 copy-start.6
  86.2 3.7 %copy-start.12 = (f32[2048,512]{1,0:T(8,128)}, f32[2048,512]{1,0:T(8,128)S(1)}, u32[]{:S(2)}) copy-start(f32[2048,512]{1,0:T(8,128)S(1)} %convolution_add_fusion) | copy-start | bytes 12582916
  97.9 29.7 %all-to-all-start.3 = ((bf16[8,128,512]{2,1,0:T(8,128)(2,1)}), bf16[8,128,512]{2,1,0:T(8,128)(2,1)}, u32[]{:S(2)}, u32[]{:S(2)}) async-start(bf16[8,128,512]{2,1,0:T(8,128)(2,1)} %bitcast.139), calls=%async_computation.3 | async-start | bytes 2097152 | tf_op jit(solution)/shard_map/all_to_all | solution.py:268
  102.2 6.0 %copy-start.16 = (bf16[1024,2048]{1,0:T(8,128)(2,1)S(1)}, bf16[1024,2048]{1,0:T(8,128)(2,1)}, u32[]{:S(2)}) copy-start(bf16[1024,2048]{1,0:T(8,128)(2,1)} %get-tuple-element.28) | copy-start | bytes 12582916
  102.2 6.0 %copy-start.21 = (f32[1024,512]{1,0:T(8,128)S(1)}, f32[1024,512]{1,0:T(8,128)}, u32[]{:S(2)}) copy-start(f32[1024,512]{1,0:T(8,128)} %get-tuple-element.32) | copy-start | bytes 6291460
  102.2 6.0 %copy-start.22 = (f32[1024,512]{1,0:T(8,128)S(1)}, f32[1024,512]{1,0:T(8,128)}, u32[]{:S(2)}) copy-start(f32[1024,512]{1,0:T(8,128)} %get-tuple-element.33) | copy-start | bytes 6291460
  108.2 2.4 copy-start.2
  127.6 29.8 %all-to-all-start.1 = ((bf16[8,128,512]{2,1,0:T(8,128)(2,1)}), bf16[8,128,512]{2,1,0:T(8,128)(2,1)}, u32[]{:S(2)}, u32[]{:S(2)}) async-start(bf16[8,128,512]{2,1,0:T(8,128)(2,1)} %bitcast.136), calls=%async_computation.1 | async-start | bytes 2097152 | tf_op jit(solution)/shard_map/all_to_all | solution.py:268
  138.7 3.1 %copy-start.26 = (f32[1,4096]{1,0:T(1,128)S(1)}, f32[1,4096]{1,0:T(1,128)}, u32[]{:S(2)}) copy-start(f32[1,4096]{1,0:T(1,128)} %param.9) | copy-start | bytes 49156
  163.1 2.6 copy-start.7
  177.7 30.6 %all-to-all-start.4 = ((bf16[128,8,512]{2,0,1:T(8,128)(2,1)}), bf16[128,8,512]{2,0,1:T(8,128)(2,1)}, u32[]{:S(2)}, u32[]{:S(2)}) async-start(bf16[128,8,512]{2,0,1:T(8,128)(2,1)} %multiply_convert_fusion.2), calls=%async_computation.4 | async-start | bytes 2097152 | tf_op jit(solution)/shard_map/all_to_all | solution.py:265
  186.3 75.8 %collective-permute-start = (bf16[128,4096]{0,1:T(8,128)(2,1)}, bf16[128,4096]{0,1:T(8,128)(2,1)}, u32[]{:S(2)}, u32[]{:S(2)}) collective-permute-start(bf16[128,4096]{0,1:T(8,128)(2,1)} %get-tuple-element.39), channel_id=1, source_target_pairs={{0,16},{16,0},{1,17},{17,1},{2,18},{18,2},{3,19},{19,3},{4,20},{20... | collective-permute-start | bytes 3145736 | tf_op jit(solution)/shard_map/ppermute | solution.py:19
  186.8 54.3 %collective-permute-start.2 = (bf16[128,4096]{0,1:T(8,128)(2,1)}, bf16[128,4096]{0,1:T(8,128)(2,1)}, u32[]{:S(2)}, u32[]{:S(2)}) collective-permute-start(bf16[128,4096]{0,1:T(8,128)(2,1)} %get-tuple-element.38), channel_id=1, source_target_pairs={{0,16},{16,0},{1,17},{17,1},{2,18},{18,2},{3,19},{19,3},{4,20},{20... | collective-permute-start | bytes 3145736 | tf_op jit(solution)/shard_map/ppermute | solution.py:19
  208.4 5.0 %copy-start.17 = (bf16[1024,2048]{1,0:T(8,128)(2,1)S(1)}, bf16[1024,2048]{1,0:T(8,128)(2,1)}, u32[]{:S(2)}) copy-start(bf16[1024,2048]{1,0:T(8,128)(2,1)} %get-tuple-element.28) | copy-start | bytes 12582916
  213.4 4.0 %copy-start.5 = (f32[2048,512]{1,0:T(8,128)S(1)}, f32[2048,512]{1,0:T(8,128)}, u32[]{:S(2)}) copy-start(f32[2048,512]{1,0:T(8,128)} %get-tuple-element.43) | copy-start | bytes 12582916
  213.4 4.0 %copy-start.13 = (f32[2048,512]{1,0:T(8,128)S(1)}, f32[2048,512]{1,0:T(8,128)}, u32[]{:S(2)}) copy-start(f32[2048,512]{1,0:T(8,128)} %copy-done.12) | copy-start | bytes 12582916
  220.3 4.8 %copy-start.8 = (f32[1024,512]{1,0:T(8,128)}, f32[1024,512]{1,0:T(8,128)S(1)}, u32[]{:S(2)}) copy-start(f32[1024,512]{1,0:T(8,128)S(1)} %get-tuple-element.31) | copy-start | bytes 6291460
  221.6 2.2 copy-start.3
  229.3 18.7 %all-to-all-start.5 = ((bf16[8,128,256]{1,2,0:T(8,128)(2,1)}), bf16[8,128,256]{1,2,0:T(8,128)(2,1)}, u32[]{:S(2)}, u32[]{:S(2)}) async-start(bf16[8,128,256]{1,2,0:T(8,128)(2,1)} %copy.30), calls=%async_computation.5 | async-start | bytes 1048576 | tf_op jit(solution)/shard_map/all_to_all | solution.py:268
  233.6 3.6 %copy-start.4 = (bf16[1024,2048]{1,0:T(8,128)(2,1)S(1)}, bf16[1024,2048]{1,0:T(8,128)(2,1)}, u32[]{:S(2)}) copy-start(bf16[1024,2048]{1,0:T(8,128)(2,1)} %get-tuple-element.29) | copy-start | bytes 12582916
  233.6 4.1 %copy-start.9 = (f32[1024,512]{1,0:T(8,128)S(1)}, f32[1024,512]{1,0:T(8,128)}, u32[]{:S(2)}) copy-start(f32[1024,512]{1,0:T(8,128)} %copy-done.8) | copy-start | bytes 6291460
  241.1 10.4 %copy-start.19 = (f32[1024,512]{1,0:T(8,128)S(1)}, f32[1024,512]{1,0:T(8,128)}, u32[]{:S(2)}) copy-start(f32[1024,512]{1,0:T(8,128)} %get-tuple-element.20) | copy-start | bytes 6291460
  247.9 18.1 %all-to-all-start.6 = ((bf16[8,128,256]{1,2,0:T(8,128)(2,1)}), bf16[8,128,256]{1,2,0:T(8,128)(2,1)S(1)}, u32[]{:S(2)}, u32[]{:S(2)}) async-start(bf16[8,128,256]{1,2,0:T(8,128)(2,1)} %copy.31), calls=%async_computation.6 | async-start | bytes 1048576 | tf_op jit(solution)/shard_map/all_to_all | solution.py:268
  251.5 6.7 %copy-start.18 = (bf16[1024,2048]{1,0:T(8,128)(2,1)S(1)}, bf16[1024,2048]{1,0:T(8,128)(2,1)}, u32[]{:S(2)}) copy-start(bf16[1024,2048]{1,0:T(8,128)(2,1)} %get-tuple-element.28) | copy-start | bytes 12582916
  251.5 6.7 %copy-start.20 = (f32[1024,512]{1,0:T(8,128)S(1)}, f32[1024,512]{1,0:T(8,128)}, u32[]{:S(2)}) copy-start(f32[1024,512]{1,0:T(8,128)} %get-tuple-element.21) | copy-start | bytes 6291460
  262.0 15.1 %collective-permute-start.4 = (bf16[128,2048]{0,1:T(8,128)(2,1)}, bf16[128,2048]{0,1:T(8,128)(2,1)S(1)}, u32[]{:S(2)}, u32[]{:S(2)}) collective-permute-start(bf16[128,2048]{0,1:T(8,128)(2,1)} %bitcast.28), channel_id=1, source_target_pairs={{0,16},{16,0},{1,17},{17,1},{2,18},{18,2},{3,19},{19,3},{4,20},{20... | collective-permute-start | bytes 1572872 | tf_op jit(solution)/shard_map/ppermute | solution.py:19
  266.1 21.0 %collective-permute-start.3 = (bf16[128,2048]{0,1:T(8,128)(2,1)S(1)}, bf16[128,2048]{0,1:T(8,128)(2,1)}, u32[]{:S(2)}, u32[]{:S(2)}) collective-permute-start(bf16[128,2048]{0,1:T(8,128)(2,1)S(1)} %bitcast.142), channel_id=1, source_target_pairs={{0,16},{16,0},{1,17},{17,1},{2,18},{18,2},{3,19},{19,3},{4,20},{20... | collective-permute-start | bytes 1572872 | tf_op jit(solution)/shard_map/ppermute | solution.py:19
